TPU v7x, 256 devices: a whole 4x4x8 slice. The times are simulated.
256 devices in a mesh: comp: 2 (over core), seq: 16 (over y_lo, z), tp: 8 (over y_hi, x).
Axes of the slice: x: 4, y: 4 (y_hi: 2, y_lo: 2; y = y_hi * 2 + y_lo), z: 8, core: 2. Of those that a mesh axis runs over, the one named last changes fastest.
Arguments:
- inputs: bfloat16 [2, 8, 2048, 3072], P('comp', None, ('seq', 'tp')), may hold values from -6 to 6
- modulation: float32 [2, 8, 3, 3072], P('comp'), may hold values from -4 to 4
- w_qkv: bfloat16 [2, 3072, 3, 3072], P('comp', None, None, 'tp'), may hold values from -0.108253175 to 0.108253175
- w_attn_out: bfloat16 [2, 3072, 3072], P('comp', 'tp'), may hold values from -0.109375 to 0.109375
- qk_gain: float32 [2, 2, 128], P('comp'), may hold values from 1 to 5
- final_mod: float32 [8, 2, 3072], replicated, may hold values from -4 to 4
- w_final: bfloat16 [3072, 64], replicated, may hold values from -0.109375 to 0.109375
- w_embed: bfloat16 [64, 3072], replicated, may hold values from -0.75 to 0.75
- latent: float32 [8, 64, 2048], P(None, None, ('seq', 'tp')), may hold values from -6 to 6
Outputs:
- handed: bfloat16 [2, 8, 2048, 3072], P('comp', None, ('seq', 'tp'))
- velocity: float32 [8, 64, 2048], P(None, None, ('seq', 'tp'))
- advanced: float32 [8, 64, 2048], P(None, None, ('seq', 'tp'))
All inputs are finite; a program needn't handle non-finite values.
Results may differ from a plain program's by a relative error of at most 0.011.
Values may be sent and summed in bfloat16 or wider, within the bound.
No kernel may reach another device: no remote copies, remote signals or barrier semaphores. Data moves between devices by JAX's collectives and lax.ppermute only.
A program may use at most 192 MiB of HBM per device.

v0:
```python
import jax
import jax.numpy as jnp
from jax import lax
from jax.sharding import PartitionSpec as P

step_size = 0.02
norm_eps = 1e-06


def broadcast(block, axis, owner):
    block = jnp.where(lax.axis_index(axis) == owner, block, jnp.zeros_like(block))
    return lax.psum(block, axis)


def shifted(block, axis, distance):
    devices = range(lax.axis_size(axis))
    route = [((i - distance) % len(devices), i) for i in devices]
    return lax.ppermute(block, axis, route)


def layer_norm(values):
    center = values - jnp.mean(values, -1, keepdims=True)
    return center * lax.rsqrt(jnp.mean(center * center, -1, keepdims=True) + norm_eps)


def rms_norm(values, norm_gain):
    return values * lax.rsqrt(jnp.mean(values * values, -1, keepdims=True) + norm_eps) * norm_gain


def body(inputs, modulation, w_qkv, w_attn_out, qk_gain, final_mod, w_final, w_embed, latent):
    head_dim = qk_gain.shape[2]
    x_rows = inputs[0]
    samples = x_rows.shape[0]
    mod_rows = modulation[0]
    x_float = x_rows.astype(jnp.float32)
    x_mod = (
        layer_norm(x_float) * (1.0 + mod_rows[:, 1, None, :]) + mod_rows[:, 0, None, :]
    ).astype(jnp.bfloat16)
    weights = w_qkv[0]
    local_width = weights.shape[2]
    heads_local = local_width // head_dim
    norm_gains = qk_gain[0]
    scaling = head_dim ** (-0.5)
    mixed_rows = jnp.einsum(
        "srd,dje->srje",
        lax.all_gather(x_mod, "tp", axis=1, tiled=True),
        weights,
        preferred_element_type=jnp.float32,
    )
    unpacked = mixed_rows.reshape(
        mixed_rows.shape[0], mixed_rows.shape[1], 3, heads_local, head_dim
    )
    project_queried = rms_norm(unpacked[:, :, 0], norm_gains[0])
    keyed_rows = rms_norm(unpacked[:, :, 1], norm_gains[1])
    projected = jnp.stack([project_queried, keyed_rows, unpacked[:, :, 2]], 2).astype(jnp.bfloat16)
    queried = projected[:, :, 0]
    query_count = queried.shape[1]
    pairs = projected[:, :, 1:]
    start_max = jnp.full((samples, query_count, heads_local), -1e30, jnp.float32)
    shard_piece = lax.all_gather(pairs, "seq", axis=1, tiled=True)
    run_max = start_max
    scores = (
        jnp.einsum(
            "sqhd,skhd->sqhk", queried, shard_piece[:, :, 0], preferred_element_type=jnp.float32
        )
        * scaling
    )
    new_max = jnp.maximum(run_max, jnp.max(scores, -1))
    weight = jnp.exp(scores - new_max[..., None])
    run_sum = jnp.sum(weight, -1)
    summed = jnp.einsum(
        "sqhk,skhd->sqhd",
        weight.astype(jnp.bfloat16),
        shard_piece[:, :, 1],
        preferred_element_type=jnp.float32,
    )
    run_acc = summed
    run_max, run_sum, run_acc = (new_max, run_sum, run_acc)
    attended = (
        (run_acc / run_sum[..., None])
        .astype(jnp.bfloat16)
        .reshape(samples, query_count, local_width)
    )
    partial_out = jnp.einsum(
        "sqe,ed->sqd", attended, w_attn_out[0], preferred_element_type=jnp.float32
    )
    branch = lax.psum_scatter(
        partial_out.astype(jnp.bfloat16), "tp", scatter_dimension=1, tiled=True
    ).astype(jnp.float32)
    output = (x_float + mod_rows[:, 2, None, :] * branch).astype(jnp.bfloat16)
    final_in = (
        layer_norm(output.astype(jnp.float32)) * (1.0 + final_mod[:, 1, None, :])
        + final_mod[:, 0, None, :]
    ).astype(jnp.bfloat16)
    velocity = jnp.einsum("srd,dc->scr", final_in, w_final, preferred_element_type=jnp.float32)
    advanced = latent + step_size * velocity
    last_comp = lax.axis_size("comp") - 1
    position = lax.axis_index("comp")
    shared = broadcast(
        jnp.stack([velocity, advanced]).astype(jnp.bfloat16), "comp", last_comp
    ).astype(jnp.float32)
    embedded = jnp.einsum(
        "scr,cd->srd", advanced.astype(jnp.bfloat16), w_embed, preferred_element_type=jnp.float32
    ).astype(jnp.bfloat16)
    sending = jnp.where(position == last_comp, embedded, output)
    handed = shifted(sending, "comp", 1)
    return (handed[None], shared[0], shared[1])


def solution(mesh):
    in_specs = (
        P("comp", None, ("seq", "tp"), None),
        P("comp", None, None, None),
        P("comp", None, None, "tp"),
        P("comp", "tp", None),
        P("comp", None, None),
        P(),
        P(),
        P(),
        P(None, None, ("seq", "tp")),
    )
    out_specs = (
        P("comp", None, ("seq", "tp"), None),
        P(None, None, ("seq", "tp")),
        P(None, None, ("seq", "tp")),
    )
    return jax.shard_map(body, mesh=mesh, in_specs=in_specs, out_specs=out_specs, check_vma=False)
```

profile of v0, /device:TPU:1, one launch (start us, length us, event | category | flops | bytes accessed | tf_op | source)
XLA Modules:
  0.0 560.2 jit_solution(11027929013083755858)
XLA Ops:
  7.2 0.0 copy-start
  7.2 0.0 copy-start.1
  7.2 0.0 all-gather.3.cloned.1.call-start
  7.2 1.2 slice_bitcast_fusion.7
  8.4 1.3 convert_reduce_fusion.1
  9.8 0.0 copy-done.1
  9.8 0.3 fusion.22
  10.1 1.3 fusion.25
  11.4 0.0 all-gather.3.cloned.1.call-update
  11.5 0.0 copy-start.5
  11.5 0.0 all-gather.5.cloned.1.call-start
  11.5 10.3 %copy.18 = bf16[1,3072,3,384]{1,3,2,0:T(8,128)(2,1)} copy(bf16[1,3072,3,384]{3,1,2,0:T(8,128)(2,1)} %param.11) | data formatting | bytes 14155776 | tf_op args[2]
  21.8 0.0 copy-done.5
  21.8 87.1 %all-gather.3.cloned.1.call-done = bf16[8,128,3072]{2,1,0:T(8,128)(2,1)} async-done(((bf16[8,16,3072]{2,1,0:T(8,128)(2,1)}), bf16[8,128,3072]{2,1,0:T(8,128)(2,1)}) %all-gather.3.cloned.1.call-update) | async-done | bytes 6291472 | tf_op jit(solution)/shard_map/all_gather | solution.py:46
  108.9 10.5 %fusion.8 = f32[8,128,3,3,128]{1,4,3,2,0:T(8,128)S(1)} fusion(bf16[3,3,128,3072,1]{3,2,1,0,4:T(8,128)(2,1)} %bitcast.110, bf16[8,128,3072]{2,1,0:T(8,128)(2,1)} %all-gather.3.cloned.1.call-done), kind=kOutput, calls=%fused_computation.11 | convolution fusion | flops 7247757312 | bytes 18087936 | tf_op jit(solution)/shard_map/srd,dje->srje/dot_general | solution.py:44
  119.4 0.0 copy-start.2
  119.4 0.4 multiply_reduce_fusion
  119.8 0.1 slice.102
  120.0 1.6 copy-done.2
  121.6 0.3 multiply_convert_fusion.1
  121.9 1.4 pad_maximum_fusion
  123.3 0.0 all-gather.5.cloned.1.call-update
  123.3 0.2 reduce-scatter.2.cloned.1.call-start
  123.6 264.5 %all-gather.5.cloned.1.call-done = bf16[8,2048,2,3,128]{1,4,3,2,0:T(8,128)(2,1)} async-done(((bf16[8,128,2,3,128]{1,4,3,2,0:T(8,128)(2,1)}), bf16[8,2048,2,3,128]{1,4,3,2,0:T(8,128)(2,1)}) %all-gather.5.cloned.1.call-update) | async-done | bytes 25165840 | tf_op jit(solution)/shard_map/all_gather | solution.py:60
  388.0 13.9 %bitcast_reduce_fusion = (f32[8,128,3]{1,2,0:T(4,128)S(1)}, f32[8,3,2048,128]{3,2,1,0:T(8,128)}) fusion(f32[8,128,3,3,128]{1,4,3,2,0:T(8,128)} %copy-done.2, f32[128]{0:T(128)S(1)} %get-tuple-element.14, f32[8,128,3]{1,2,0:T(4,128)S(1)} %add_rsqrt_fusion, bf16[8,2048,2,3,128]{1,4,3,2,0:T(8,128)(2,1)} %all-gather.5.cloned.1.call-done), kind=kOutput, calls=%fused_computation.1 | convolution fusion | flops 1624372224 | bytes 39346688 | tf_op jit(solution)/shard_map/sqhd,skhd->sqhk/dot_general | solution.py:63
  402.0 10.5 %fusion.1 = f32[8,128,3]{1,2,0:T(4,128)S(1)} fusion(f32[8,3,2048,128]{3,2,1,0:T(8,128)} %get-tuple-element.17, f32[8,128,3]{1,2,0:T(4,128)S(1)} %broadcast_maximum_fusion), kind=kLoop, calls=%fused_computation.3 | loop fusion | flops 18871296 | bytes 25190400 | tf_op jit(solution)/shard_map/reduce_sum | solution.py:70
  412.4 15.2 %fusion.27 = bf16[8,128,3,128]{1,3,2,0:T(8,128)(2,1)S(1)} fusion(f32[8,3,2048,128]{3,2,1,0:T(8,128)} %get-tuple-element.17, f32[8,128,3]{1,2,0:T(4,128)S(1)} %broadcast_maximum_fusion, bf16[8,2048,2,3,128]{1,4,3,2,0:T(8,128)(2,1)} %all-gather.5.cloned.1.call-done, f32[8,128,3]{1,2,0:T(4,128)S(1)} %fusion.1), kind=kOutput, calls=%fused_computation.39 | convolution fusion | flops 1630273536 | bytes 38559744 | tf_op jit(solution)/shard_map/sqhk,skhd->sqhd/dot_general | solution.py:71
  427.6 0.0 copy-done
  427.6 5.4 convolution_convert_fusion
  433.0 0.0 copy-start.4
  433.0 0.0 reduce-scatter.2.cloned.1.call-update
  433.1 0.9 copy-done.4
  433.9 0.2 fusion.43
  434.2 108.9 %reduce-scatter.2.cloned.1.call-done = bf16[8,16,3072]{2,1,0:T(8,128)(2,1)} async-done(((bf16[8,128,3072]{2,1,0:T(8,128)(2,1)}), bf16[8,16,3072]{2,1,0:T(8,128)(2,1)}) %reduce-scatter.2.cloned.1.call-update) | async-done | bytes 786448 | tf_op jit(solution)/shard_map/reduce_scatter | solution.py:87
  543.1 0.0 copy-start.6
  543.1 1.5 convert_reduce_fusion
  544.6 0.0 copy-start.3
  544.7 0.3 fusion.18
  545.0 0.0 copy-done.6
  545.0 0.0 copy-done.7
  545.0 0.5 fusion.40
  545.5 0.1 copy-done.3
  545.6 1.2 fusion.10
  546.9 1.6 collective-permute-start
  548.5 3.6 psum.7
  552.1 0.7 slice_bitcast_fusion.8
  552.8 0.0 collective-permute-done
  552.8 0.9 copy.37
  (12 shorter events, 0.1 us)
Async XLA Ops:
  7.2 420.4 %copy-start = (bf16[1,384,3072]{2,1,0:T(8,128)(2,1)S(1)}, bf16[1,384,3072]{2,1,0:T(8,128)(2,1)}, u32[]{:S(2)}) copy-start(bf16[1,384,3072]{2,1,0:T(8,128)(2,1)} %param.12) | copy-start | bytes 7077892
  7.2 2.6 copy-start.1
  7.2 101.7 %all-gather.3.cloned.1.call-start = ((), (), s32[]{:S(2)}) async-start(), calls=%async_computation.1 | async-start | bytes 7077888 | tf_op jit(solution)/shard_map/all_gather | solution.py:46
  11.5 10.3 %copy-start.5 = (f32[1,2,128]{2,1,0:T(2,128)S(1)}, f32[1,2,128]{2,1,0:T(2,128)}, u32[]{:S(2)}) copy-start(f32[1,2,128]{2,1,0:T(2,128)} %param.13) | copy-start | bytes 3076
  11.5 376.6 %all-gather.5.cloned.1.call-start = ((), (), s32[]{:S(2)}) async-start(), calls=%async_computation.2 | async-start | bytes 26738688 | tf_op jit(solution)/shard_map/all_gather | solution.py:60
  119.4 2.2 copy-start.2
  123.3 419.8 %reduce-scatter.2.cloned.1.call-start = ((), (), s32[]{:S(2)}) async-start(), calls=%async_computation.3 | async-start | bytes 7077888 | tf_op jit(solution)/shard_map/reduce_scatter | solution.py:87
  433.0 0.9 copy-start.4
  543.1 1.9 copy-start.6
  543.1 1.9 copy-start.7
  544.6 1.0 copy-start.3
  546.9 5.9 %collective-permute-start = (bf16[8,16,3072]{2,1,0:T(8,128)(2,1)}, bf16[8,16,3072]{2,1,0:T(8,128)(2,1)S(1)}, u32[]{:S(2)}, u32[]{:S(2)}) collective-permute-start(bf16[8,16,3072]{2,1,0:T(8,128)(2,1)} %fusion.10), channel_id=1, source_target_pairs={{128,0},{0,128},{129,1},{1,129},{130,2},{2,130},{131,3},{3,131},{1... | collective-permute-start | bytes 2359304 | tf_op jit(solution)/shard_map/ppermute | solution.py:18
Sparse Core Ops, SparseCore 0:
  11.6 97.2 all-gather.2
  123.4 264.5 all-gather.4
  433.2 109.8 reduce-scatter.1
where the time goes:
time: 561 us; the launch traced here: 560 us
  waiting for transfers between devices  461 us (82%)
  matrix products  46.8 us (8%)
  other arithmetic  18.7 us (3%)
  local copies, waits for them, and re-layouts  14.8 us (3%)
  between operations  13.9 us (2%)
    all_gather x1, waiting for transfers between devices, body(): shard_piece = lax.all_gather(pairs, 'seq', axis=1, tiled=True)  264 us
    reduce_scatter x1, waiting for transfers between devices, body(): lax.psum_scatter(partial_out.astype(jnp.bfloat16), 'tp', scatter_dimensio...  109 us
    all_gather x1, waiting for transfers between devices, body(): lax.all_gather(x_mod, 'tp', axis=1, tiled=True)  87.1 us
    dot_general x1, matrix products, body(): jnp.einsum('sqhk,skhd->sqhd', weight.astype(jnp.bfloat16), shard_piece[:,...  15.2 us
    dot_general x1, matrix products, body(): jnp.einsum('sqhd,skhd->sqhk', queried, shard_piece[:, :, 0], preferred_el...  13.9 us
    unnamed x18, local copies, waits for them, and re-layouts  13.8 us
  transfers between devices with their start and end apart: 4, of which 3 were waited for; matrix products, arithmetic and copies ran while one was open for 2% of the time, Pallas kernels for 0%

commit v1 on v0

--- a/solution.py
+++ b/solution.py
@@ -30,63 +30,72 @@
 def body(inputs, modulation, w_qkv, w_attn_out, qk_gain, final_mod, w_final, w_embed, latent):
     head_dim = qk_gain.shape[2]
     x_rows = inputs[0]
-    samples = x_rows.shape[0]
+    samples, tokens_local, width = x_rows.shape
+    n_seq = lax.axis_size("seq")
+    parts = n_seq // samples
+    part_tokens = tokens_local // parts
     mod_rows = modulation[0]
     x_float = x_rows.astype(jnp.float32)
     x_mod = (
         layer_norm(x_float) * (1.0 + mod_rows[:, 1, None, :]) + mod_rows[:, 0, None, :]
     ).astype(jnp.bfloat16)
+    x_parts = x_mod.reshape(samples * parts, part_tokens, width)
+    x_clip = lax.all_to_all(x_parts, "seq", 0, 0, tiled=True)
+    x_group = lax.all_gather(x_clip, "tp", axis=0, tiled=False)
+    n_tp, n_src = x_group.shape[0], x_group.shape[1]
+    rows = n_tp * n_src * part_tokens
     weights = w_qkv[0]
     local_width = weights.shape[2]
     heads_local = local_width // head_dim
     norm_gains = qk_gain[0]
     scaling = head_dim ** (-0.5)
     mixed_rows = jnp.einsum(
-        "srd,dje->srje",
-        lax.all_gather(x_mod, "tp", axis=1, tiled=True),
+        "rd,dje->rje",
+        x_group.reshape(rows, width),
         weights,
         preferred_element_type=jnp.float32,
     )
-    unpacked = mixed_rows.reshape(
-        mixed_rows.shape[0], mixed_rows.shape[1], 3, heads_local, head_dim
-    )
-    project_queried = rms_norm(unpacked[:, :, 0], norm_gains[0])
-    keyed_rows = rms_norm(unpacked[:, :, 1], norm_gains[1])
-    projected = jnp.stack([project_queried, keyed_rows, unpacked[:, :, 2]], 2).astype(jnp.bfloat16)
-    queried = projected[:, :, 0]
-    query_count = queried.shape[1]
-    pairs = projected[:, :, 1:]
-    start_max = jnp.full((samples, query_count, heads_local), -1e30, jnp.float32)
-    shard_piece = lax.all_gather(pairs, "seq", axis=1, tiled=True)
-    run_max = start_max
+    unpacked = mixed_rows.reshape(rows, 3, heads_local, head_dim)
+    queried = rms_norm(unpacked[:, 0], norm_gains[0]).astype(jnp.bfloat16)
+    keyed_rows = rms_norm(unpacked[:, 1], norm_gains[1]).astype(jnp.bfloat16)
+    pairs = jnp.stack([keyed_rows, unpacked[:, 2].astype(jnp.bfloat16)], 0)
+    partner = [(i, i ^ 1) for i in range(n_seq)]
+    other = lax.ppermute(pairs, "seq", partner)
+    all_pairs = jnp.concatenate([pairs, other], 1)
     scores = (
         jnp.einsum(
-            "sqhd,skhd->sqhk", queried, shard_piece[:, :, 0], preferred_element_type=jnp.float32
+            "qhd,khd->hqk", queried, all_pairs[0], preferred_element_type=jnp.float32
         )
         * scaling
     )
-    new_max = jnp.maximum(run_max, jnp.max(scores, -1))
-    weight = jnp.exp(scores - new_max[..., None])
-    run_sum = jnp.sum(weight, -1)
+    row_max = jnp.max(scores, -1)
+    weight = jnp.exp(scores - row_max[..., None])
+    row_sum = jnp.sum(weight, -1)
     summed = jnp.einsum(
-        "sqhk,skhd->sqhd",
+        "hqk,khd->qhd",
         weight.astype(jnp.bfloat16),
-        shard_piece[:, :, 1],
+        all_pairs[1],
         preferred_element_type=jnp.float32,
     )
-    run_acc = summed
-    run_max, run_sum, run_acc = (new_max, run_sum, run_acc)
     attended = (
-        (run_acc / run_sum[..., None])
+        (summed / jnp.transpose(row_sum)[..., None])
         .astype(jnp.bfloat16)
-        .reshape(samples, query_count, local_width)
+        .reshape(rows, local_width)
     )
     partial_out = jnp.einsum(
-        "sqe,ed->sqd", attended, w_attn_out[0], preferred_element_type=jnp.float32
+        "re,ed->rd", attended, w_attn_out[0], preferred_element_type=jnp.float32
     )
-    branch = lax.psum_scatter(
-        partial_out.astype(jnp.bfloat16), "tp", scatter_dimension=1, tiled=True
-    ).astype(jnp.float32)
+    branch_clip = lax.psum_scatter(
+        partial_out.astype(jnp.bfloat16).reshape(n_tp, n_src * part_tokens, width),
+        "tp",
+        scatter_dimension=0,
+        tiled=True,
+    ).reshape(n_src, part_tokens, width)
+    branch = (
+        lax.all_to_all(branch_clip, "seq", 0, 0, tiled=True)
+        .reshape(samples, tokens_local, width)
+        .astype(jnp.float32)
+    )
     output = (x_float + mod_rows[:, 2, None, :] * branch).astype(jnp.bfloat16)
     final_in = (
         layer_norm(output.astype(jnp.float32)) * (1.0 + final_mod[:, 1, None, :])

time: 561 us -> 370 us (0.66)
  waiting for transfers between devices: 461 us -> 237 us
  blocking collectives: 3.59 us -> 33.8 us
  starting transfers between devices: 1.93 us -> 12.2 us
  matrix products: 46.8 us -> 39 us
    all_gather x2 -> x1, waiting for transfers between devices: 352 us -> 83.2 us  [body(): x_group = lax.all_gather(x_clip, 'tp', axis=0, tiled=False)]
    ppermute x0 -> x1, waiting for transfers between devices: none -> 33.1 us  [body(): other = lax.ppermute(pairs, 'seq', partner)]
    all_to_all x0 -> x1, blocking collectives: none -> 30.2 us  [body(): x_clip = lax.all_to_all(x_parts, 'seq', 0, 0, tiled=True)]
    all_to_all x0 -> x1, waiting for transfers between devices: none -> 18 us  [body(): lax.all_to_all(branch_clip, 'seq', 0, 0, tiled=True)]
    dot_general x4, matrix products: 45 us -> 37.3 us  [the longest x1 10.9 us: body(): jnp.einsum('rd,dje->rje', x_group.reshape(rows, width), weights, preferre...]
    all_to_all x0 -> x1, starting transfers between devices: none -> 6.87 us  [body(): lax.all_to_all(branch_clip, 'seq', 0, 0, tiled=True)]
    reduce_scatter x1, waiting for transfers between devices: 109 us -> 103 us  [body(): lax.psum_scatter(partial_out.astype(jnp.bfloat16).reshape(n_tp, n_src * p...]
    unnamed x18 -> x20, local copies, waits for them, and re-layouts: 13.8 us -> 11.3 us
  transfers between devices with their start and end apart: 4 -> 5, of which waited for: 3 -> 4; matrix products, arithmetic and copies ran while one was open for 2% -> 3% of each run, Pallas kernels for 0% -> 0%
where the time goes in v1:
time: 370 us
  waiting for transfers between devices  237 us (64%)
  matrix products  39 us (11%)
  blocking collectives  33.8 us (9%)
  other arithmetic  18.9 us (5%)
  local copies, waits for them, and re-layouts  14.4 us (4%)
  between operations  14.3 us (4%)
  starting transfers between devices  12.2 us (3%)
    reduce_scatter x1, waiting for transfers between devices, body(): lax.psum_scatter(partial_out.astype(jnp.bfloat16).reshape(n_tp, n_src * p...  103 us
    all_gather x1, waiting for transfers between devices, body(): x_group = lax.all_gather(x_clip, 'tp', axis=0, tiled=False)  83.2 us
    ppermute x1, waiting for transfers between devices, body(): other = lax.ppermute(pairs, 'seq', partner)  33.1 us
    all_to_all x1, blocking collectives, body(): x_clip = lax.all_to_all(x_parts, 'seq', 0, 0, tiled=True)  30.2 us
    all_to_all x1, waiting for transfers between devices, body(): lax.all_to_all(branch_clip, 'seq', 0, 0, tiled=True)  18 us
    unnamed x20, local copies, waits for them, and re-layouts  11.3 us
    dot_general x1, matrix products, body(): jnp.einsum('rd,dje->rje', x_group.reshape(rows, width), weights, preferre...  10.9 us
    reduce_sum x1, other arithmetic, body(): row_sum = jnp.sum(weight, -1)  10.8 us
  transfers between devices with their start and end apart: 5, of which 4 were waited for; matrix products, arithmetic and copies ran while one was open for 3% of the time, Pallas kernels for 0%

profile of v1, /device:TPU:1, one launch (start us, length us, event | category | flops | bytes accessed | tf_op | source)
XLA Modules:
  0.0 369.5 jit_solution(10017605705453183424)
XLA Ops:
  7.2 0.0 copy-start
  7.2 0.0 all-gather.3.cloned.1.call-start
  7.2 1.5 convert_reduce_fusion.1
  8.7 1.5 fusion.21
  10.3 0.1 div.29
  10.4 0.7 slice_bitcast_fusion.6
  11.1 0.1 add.77
  11.1 0.1 add.78
  11.3 1.0 mul.133
  12.3 0.8 mul.134
  13.1 0.1 rsqrt.36
  13.1 1.3 add_convert_fusion
  14.5 30.2 %all_to_all.10 = bf16[16,8,3072]{2,1,0:T(8,128)(2,1)} all-to-all(bf16[16,8,3072]{2,1,0:T(8,128)(2,1)S(1)} %add_convert_fusion), channel_id=1, replica_groups=mesh['comp'=2,'seq'=16,'tp'=8] {'seq'}, dimensions={0} | all-to-all | bytes 1572864 | tf_op jit(solution)/shard_map/all_to_all | solution.py:43
  44.7 0.0 all-gather.3.cloned.1.call-update
  44.7 0.0 copy-start.6
  44.7 0.0 reduce-scatter.2.cloned.1.call-start
  44.8 10.3 %copy.21 = bf16[1,3072,3,384]{1,3,2,0:T(8,128)(2,1)} copy(bf16[1,3072,3,384]{3,1,2,0:T(8,128)(2,1)} %param.11) | data formatting | bytes 14155776 | tf_op args[2]
  55.0 83.2 %all-gather.3.cloned.1.call-done = bf16[128,8,3072]{2,1,0:T(8,128)(2,1)} async-done(((bf16[16,8,3072]{2,1,0:T(8,128)(2,1)}), bf16[128,8,3072]{2,1,0:T(8,128)(2,1)}) %all-gather.3.cloned.1.call-update) | async-done | bytes 6291472 | tf_op jit(solution)/shard_map/all_gather | solution.py:44
  138.3 10.9 %fusion.4 = f32[1024,3,3,128]{0,3,2,1:T(8,128)S(1)} fusion(bf16[3,3,128,3072]{3,2,1,0:T(8,128)(2,1)} %bitcast.106, bf16[128,8,3072]{2,1,0:T(8,128)(2,1)} %all-gather.3.cloned.1.call-done), kind=kOutput, calls=%fused_computation.5 | convolution fusion | flops 7247757312 | bytes 18087936 | tf_op jit(solution)/shard_map/rd,dje->rje/dot_general | solution.py:52
  149.2 0.1 fusion.22
  149.3 0.2 multiply_reduce_fusion.2
  149.5 0.3 fusion.19
  149.8 0.1 pad_maximum_fusion.1
  150.0 1.5 collective-permute-start
  151.5 0.2 multiply_reduce_fusion.1
  151.7 33.1 %collective-permute-done = bf16[2,1024,3,128]{1,3,2,0:T(8,128)(2,1)S(1)} collective-permute-done((bf16[2,1024,3,128]{1,3,2,0:T(8,128)(2,1)S(1)}, bf16[2,1024,3,128]{1,3,2,0:T(8,128)(2,1)S(1)}, u32[]{:S(2)}, u32[]{:S(2)}) %collective-permute-start) | collective-permute-done | bytes 1572896 | tf_op jit(solution)/shard_map/ppermute | solution.py:63
  184.8 0.3 pad_maximum_fusion
  185.1 10.2 %multiply_reduce_fusion = (f32[3,1024]{1,0:T(4,128)S(1)}, f32[3,1024,2048]{2,1,0:T(8,128)}) fusion(bf16[2,2048,3,128]{1,3,2,0:T(8,128)(2,1)S(1)} %pad_maximum_fusion, f32[1024,3,3,128]{0,3,2,1:T(8,128)S(1)} %fusion.4, f32[128]{0:T(128)S(1)} %get-tuple-element.12, f32[1024,3]{0,1:T(4,128)S(1)} %add_rsqrt_fusion), kind=kOutput, calls=%fused_computation.1 | convolution fusion | flops 1624372224 | bytes 28340736 | tf_op jit(solution)/shard_map/qhd,khd->hqk/dot_general | solution.py:66
  195.3 10.8 %fusion = f32[3,1024]{1,0:T(4,128)S(1)} fusion(f32[3,1024,2048]{2,1,0:T(8,128)} %get-tuple-element.15, f32[3,1024]{1,0:T(4,128)S(1)} %get-tuple-element.14), kind=kLoop, calls=%fused_computation.2 | loop fusion | flops 18871296 | bytes 25190400 | tf_op jit(solution)/shard_map/reduce_sum | solution.py:73
  206.0 10.8 %fusion.17 = bf16[1024,3,128]{0,2,1:T(8,128)(2,1)S(1)} fusion(f32[1024,3]{0,1:T(4,128)S(1)} %bitcast.113, f32[3,1024,2048]{2,1,0:T(8,128)} %get-tuple-element.15, f32[3,1024]{1,0:T(4,128)S(1)} %get-tuple-element.14, bf16[2,2048,3,128]{1,3,2,0:T(8,128)(2,1)S(1)} %pad_maximum_fusion), kind=kOutput, calls=%fused_computation.30 | convolution fusion | flops 1630273536 | bytes 27557888 | tf_op jit(solution)/shard_map/hqk,khd->qhd/dot_general | solution.py:74
  216.8 5.4 %convolution_convert_fusion = bf16[1024,3072]{1,0:T(8,128)(2,1)} fusion(bf16[1024,384]{0,1:T(8,128)(2,1)S(1)} %bitcast.114, bf16[1,384,3072]{2,1,0:T(8,128)(2,1)S(1)} %copy-done), kind=kOutput, calls=%fused_computation.7 | convolution fusion | flops 2419064832 | bytes 9437184 | tf_op jit(solution)/shard_map/re,ed->rd/dot_general | solution.py:85
  222.3 0.0 reduce-scatter.2.cloned.1.call-update
  222.3 0.0 copy-start.5
  222.3 102.6 %reduce-scatter.2.cloned.1.call-done = bf16[1,128,3072]{2,1,0:T(8,128)(2,1)} async-done(((bf16[8,128,3072]{2,1,0:T(8,128)(2,1)}), bf16[1,128,3072]{2,1,0:T(8,128)(2,1)}) %reduce-scatter.2.cloned.1.call-update) | async-done | bytes 786448 | tf_op jit(solution)/shard_map/reduce_scatter | solution.py:88
  324.9 6.9 %all-to-all-start.1 = ((bf16[16,8,3072]{2,1,0:T(8,128)(2,1)}), bf16[16,8,3072]{2,1,0:T(8,128)(2,1)}, u32[]{:S(2)}, u32[]{:S(2)}) async-start(bf16[16,8,3072]{2,1,0:T(8,128)(2,1)} %bitcast.108), calls=%async_computation.2 | async-start | bytes 1572864 | tf_op jit(solution)/shard_map/all_to_all | solution.py:95
  331.8 0.2 fusion.36
  332.0 18.0 %all-to-all-done.1 = bf16[16,8,3072]{2,1,0:T(8,128)(2,1)} async-done(((bf16[16,8,3072]{2,1,0:T(8,128)(2,1)}), bf16[16,8,3072]{2,1,0:T(8,128)(2,1)}, u32[]{:S(2)}, u32[]{:S(2)}) %all-to-all-start.1) | async-done | bytes 786464 | tf_op jit(solution)/shard_map/all_to_all | solution.py:95
  350.0 1.5 convert_reduce_fusion
  351.6 0.0 copy-start.3
  351.6 0.3 fusion.10
  351.9 0.0 copy-done.8
  351.9 0.5 fusion.31
  352.5 0.1 copy-done.3
  352.6 1.2 fusion.6
  353.8 3.7 %collective-permute-start.1 = (bf16[8,16,3072]{2,1,0:T(8,128)(2,1)}, bf16[8,16,3072]{2,1,0:T(8,128)(2,1)S(1)}, u32[]{:S(2)}, u32[]{:S(2)}) collective-permute-start(bf16[8,16,3072]{2,1,0:T(8,128)(2,1)} %fusion.6), channel_id=1, source_target_pairs={{128,0},{0,128},{129,1},{1,129},{130,2},{2,130},{131,3},{3,131},{1... | collective-permute-start | bytes 2359304 | tf_op jit(solution)/shard_map/ppermute | solution.py:18
  357.5 3.6 psum.7
  361.1 0.7 slice_bitcast_fusion.7
  361.8 0.9 copy.36
  (23 shorter events, 0.2 us)
Async XLA Ops:
  7.2 209.7 %copy-start = (bf16[1,384,3072]{2,1,0:T(8,128)(2,1)S(1)}, bf16[1,384,3072]{2,1,0:T(8,128)(2,1)}, u32[]{:S(2)}) copy-start(bf16[1,384,3072]{2,1,0:T(8,128)(2,1)} %param.12) | copy-start | bytes 7077892
  7.2 3.2 copy-start.4
  7.2 131.1 %all-gather.3.cloned.1.call-start = ((), (), s32[]{:S(2)}) async-start(), calls=%async_computation.4 | async-start | bytes 7077888 | tf_op jit(solution)/shard_map/all_gather | solution.py:44
  8.7 4.4 %copy-start.1 = (bf16[1,8,16,3072]{3,2,1,0:T(8,128)(2,1)S(1)}, bf16[1,8,16,3072]{3,2,1,0:T(8,128)(2,1)}, u32[]{:S(2)}) copy-start(bf16[1,8,16,3072]{3,2,1,0:T(8,128)(2,1)} %param.9) | copy-start | bytes 2359300
  44.7 10.3 %copy-start.6 = (f32[1,2,128]{2,1,0:T(2,128)S(1)}, f32[1,2,128]{2,1,0:T(2,128)}, u32[]{:S(2)}) copy-start(f32[1,2,128]{2,1,0:T(2,128)} %param.13) | copy-start | bytes 3076
  44.7 280.2 %reduce-scatter.2.cloned.1.call-start = ((), (), s32[]{:S(2)}) async-start(), calls=%async_computation.3 | async-start | bytes 7077888 | tf_op jit(solution)/shard_map/reduce_scatter | solution.py:88
  150.0 34.8 %collective-permute-start = (bf16[2,1024,3,128]{1,3,2,0:T(8,128)(2,1)S(1)}, bf16[2,1024,3,128]{1,3,2,0:T(8,128)(2,1)S(1)}, u32[]{:S(2)}, u32[]{:S(2)}) collective-permute-start(bf16[2,1024,3,128]{1,3,2,0:T(8,128)(2,1)S(1)} %pad_maximum_fusion.1), channel_id=1, source_target_pairs={{0,8},{8,0},{16,24},{24,16},{32,40},{40,32},{48,56},{56,48},{64,72... | collective-permute-start | bytes 4718600 | tf_op jit(solution)/shard_map/ppermute | solution.py:63
  222.3 109.5 %copy-start.5 = (f32[8,2,3072]{2,1,0:T(2,128)S(1)}, f32[8,2,3072]{2,1,0:T(2,128)}, u32[]{:S(2)}) copy-start(f32[8,2,3072]{2,1,0:T(2,128)} %param.14) | copy-start | bytes 589828
  222.3 127.7 %copy-start.2 = (f32[8,3072]{1,0:T(8,128)S(1)}, f32[8,3072]{1,0:T(8,128)}, u32[]{:S(2)}) copy-start(f32[8,3072]{1,0:T(8,128)} %get-tuple-element.5) | copy-start | bytes 294916
  324.9 25.1 %all-to-all-start.1 = ((bf16[16,8,3072]{2,1,0:T(8,128)(2,1)}), bf16[16,8,3072]{2,1,0:T(8,128)(2,1)}, u32[]{:S(2)}, u32[]{:S(2)}) async-start(bf16[16,8,3072]{2,1,0:T(8,128)(2,1)} %bitcast.108), calls=%async_computation.2 | async-start | bytes 1572864 | tf_op jit(solution)/shard_map/all_to_all | solution.py:95
  350.0 1.9 copy-start.7
  350.0 1.9 copy-start.8
  351.6 1.0 copy-start.3
  353.8 8.0 %collective-permute-start.1 = (bf16[8,16,3072]{2,1,0:T(8,128)(2,1)}, bf16[8,16,3072]{2,1,0:T(8,128)(2,1)S(1)}, u32[]{:S(2)}, u32[]{:S(2)}) collective-permute-start(bf16[8,16,3072]{2,1,0:T(8,128)(2,1)} %fusion.6), channel_id=1, source_target_pairs={{128,0},{0,128},{129,1},{1,129},{130,2},{2,130},{131,3},{3,131},{1... | collective-permute-start | bytes 2359304 | tf_op jit(solution)/shard_map/ppermute | solution.py:18
Sparse Core Ops, SparseCore 0:
  44.8 93.4 all-gather.2
  222.4 102.4 reduce-scatter.1

commit v2 on v1

--- a/solution.py
+++ b/solution.py
@@ -1,6 +1,9 @@
 import jax
 import jax.numpy as jnp
 from jax import lax
+import functools
+from jax.experimental import pallas as pl
+from jax.experimental.pallas import tpu as pltpu
 from jax.sharding import PartitionSpec as P
 
 step_size = 0.02
@@ -27,6 +30,81 @@
     return values * lax.rsqrt(jnp.mean(values * values, -1, keepdims=True) + norm_eps) * norm_gain
 
 
+def _project_kernel(x_ref, w_ref, g_ref, o_ref, *, heads):
+    which = pl.program_id(0) // heads
+    mixed = jnp.dot(x_ref[...], w_ref[...], preferred_element_type=jnp.float32)
+    normed = (
+        mixed
+        * lax.rsqrt(jnp.mean(mixed * mixed, -1, keepdims=True) + norm_eps)
+        * g_ref[pl.ds(which, 1), :]
+    )
+    o_ref[...] = jnp.where(which < 2, normed, mixed).astype(o_ref.dtype)
+
+
+def project(x, w, gains, head_dim):
+    rows, width = x.shape
+    local_width = w.shape[2]
+    heads = local_width // head_dim
+    kernel = functools.partial(_project_kernel, heads=heads)
+    return pl.pallas_call(
+        kernel,
+        grid=(3 * heads,),
+        in_specs=[
+            pl.BlockSpec((rows, width), lambda c: (0, 0)),
+            pl.BlockSpec((None, width, head_dim), lambda c: (c // heads, 0, c % heads)),
+            pl.BlockSpec(gains.shape, lambda c: (0, 0)),
+        ],
+        out_specs=pl.BlockSpec(
+            (None, rows, head_dim), lambda c: (c // heads, 0, c % heads)
+        ),
+        out_shape=jax.ShapeDtypeStruct((3, rows, local_width), jnp.bfloat16),
+        compiler_params=pltpu.CompilerParams(vmem_limit_bytes=48 * 1024 * 1024),
+    )(x, w, gains)
+
+
+def _attend_kernel(q_ref, k_ref, v_ref, ko_ref, vo_ref, o_ref, *, scaling):
+    def scores_of(keys):
+        return lax.dot_general(
+            q_ref[...], keys[...], (((1,), (1,)), ((), ())), preferred_element_type=jnp.float32
+        ) * scaling
+
+    own = scores_of(k_ref)
+    far = scores_of(ko_ref)
+    row_max = jnp.maximum(jnp.max(own, -1, keepdims=True), jnp.max(far, -1, keepdims=True))
+    own = jnp.exp(own - row_max)
+    far = jnp.exp(far - row_max)
+    row_sum = jnp.sum(own, -1, keepdims=True) + jnp.sum(far, -1, keepdims=True)
+    summed = jnp.dot(
+        own.astype(jnp.bfloat16), v_ref[...], preferred_element_type=jnp.float32
+    ) + jnp.dot(far.astype(jnp.bfloat16), vo_ref[...], preferred_element_type=jnp.float32)
+    o_ref[...] = (summed / row_sum).astype(o_ref.dtype)
+
+
+def attend(qkv, other, head_dim, block_q=512):
+    rows, width = qkv.shape[1], qkv.shape[2]
+    keys = other.shape[1]
+    heads = width // head_dim
+    kernel = functools.partial(_attend_kernel, scaling=head_dim ** (-0.5))
+
+    def part(index, extent):
+        return pl.BlockSpec((None, extent, head_dim), lambda h, i: (index, 0, h))
+
+    return pl.pallas_call(
+        kernel,
+        grid=(heads, rows // block_q),
+        in_specs=[
+            pl.BlockSpec((None, block_q, head_dim), lambda h, i: (0, i, h)),
+            part(1, rows),
+            part(2, rows),
+            part(0, keys),
+            part(1, keys),
+        ],
+        out_specs=pl.BlockSpec((block_q, head_dim), lambda h, i: (i, h)),
+        out_shape=jax.ShapeDtypeStruct((rows, width), jnp.bfloat16),
+        compiler_params=pltpu.CompilerParams(vmem_limit_bytes=48 * 1024 * 1024),
+    )(qkv, qkv, qkv, other, other)
+
+
 def body(inputs, modulation, w_qkv, w_attn_out, qk_gain, final_mod, w_final, w_embed, latent):
     head_dim = qk_gain.shape[2]
     x_rows = inputs[0]
@@ -48,40 +126,13 @@
     local_width = weights.shape[2]
     heads_local = local_width // head_dim
     norm_gains = qk_gain[0]
-    scaling = head_dim ** (-0.5)
-    mixed_rows = jnp.einsum(
-        "rd,dje->rje",
-        x_group.reshape(rows, width),
-        weights,
-        preferred_element_type=jnp.float32,
+    gains = jnp.concatenate([norm_gains, jnp.ones_like(norm_gains[:1])], 0)
+    qkv = project(
+        x_group.reshape(rows, width), jnp.transpose(weights, (1, 0, 2)), gains, head_dim
     )
-    unpacked = mixed_rows.reshape(rows, 3, heads_local, head_dim)
-    queried = rms_norm(unpacked[:, 0], norm_gains[0]).astype(jnp.bfloat16)
-    keyed_rows = rms_norm(unpacked[:, 1], norm_gains[1]).astype(jnp.bfloat16)
-    pairs = jnp.stack([keyed_rows, unpacked[:, 2].astype(jnp.bfloat16)], 0)
     partner = [(i, i ^ 1) for i in range(n_seq)]
-    other = lax.ppermute(pairs, "seq", partner)
-    all_pairs = jnp.concatenate([pairs, other], 1)
-    scores = (
-        jnp.einsum(
-            "qhd,khd->hqk", queried, all_pairs[0], preferred_element_type=jnp.float32
-        )
-        * scaling
-    )
-    row_max = jnp.max(scores, -1)
-    weight = jnp.exp(scores - row_max[..., None])
-    row_sum = jnp.sum(weight, -1)
-    summed = jnp.einsum(
-        "hqk,khd->qhd",
-        weight.astype(jnp.bfloat16),
-        all_pairs[1],
-        preferred_element_type=jnp.float32,
-    )
-    attended = (
-        (summed / jnp.transpose(row_sum)[..., None])
-        .astype(jnp.bfloat16)
-        .reshape(rows, local_width)
-    )
+    other = lax.ppermute(qkv[1:], "seq", partner)
+    attended = attend(qkv, other, head_dim)
     partial_out = jnp.einsum(
         "re,ed->rd", attended, w_attn_out[0], preferred_element_type=jnp.float32
     )

time: 370 us -> 366 us (0.989)
  Pallas kernels: 0 us -> 39.5 us
  matrix products: 39 us -> 7.15 us
  other arithmetic: 18.9 us -> 7.02 us
  local copies, waits for them, and re-layouts: 14.4 us -> 4.13 us
  waiting for transfers between devices: 237 us -> 247 us
    pallas_call x0 -> x2, Pallas kernels: none -> 39.5 us  [the longest x1 20.5 us: project(): pl.pallas_call(kernel, grid=(3 * heads,), in_specs=[pl.BlockSpec((rows, w...]
    dot_general x3 -> x0, matrix products: 31.8 us -> none  [the longest x1 10.9 us: body(): jnp.einsum('rd,dje->rje', x_group.reshape(rows, width), weights, preferre...]
    reduce_sum x3 -> x0, other arithmetic: 11.1 us -> none  [the longest x1 10.8 us: body(): row_sum = jnp.sum(weight, -1)]
    unnamed x20 -> x19, local copies, waits for them, and re-layouts: 11.3 us -> 1.04 us
    all_gather x1, waiting for transfers between devices: 83.2 us -> 93.5 us  [body(): x_group = lax.all_gather(x_clip, 'tp', axis=0, tiled=False)]
  transfers between devices with their start and end apart: 5 -> 5, of which waited for: 4 -> 4; matrix products, arithmetic and copies ran while one was open for 3% -> 0% of each run, Pallas kernels for 0% -> 0%
where the time goes in v2:
time: 366 us; the launch traced here: 365 us
  waiting for transfers between devices  247 us (67%)
  Pallas kernels  39.5 us (11%)
  blocking collectives  33.8 us (9%)
  between operations  14.3 us (4%)
  starting transfers between devices  12.1 us (3%)
  matrix products  7.15 us (2%)
  other arithmetic  7.02 us (2%)
  local copies, waits for them, and re-layouts  4.13 us (1%)
    reduce_scatter x1, waiting for transfers between devices, body(): lax.psum_scatter(partial_out.astype(jnp.bfloat16).reshape(n_tp, n_src * p...  103 us
    all_gather x1, waiting for transfers between devices, body(): x_group = lax.all_gather(x_clip, 'tp', axis=0, tiled=False)  93.5 us
    ppermute x1, waiting for transfers between devices, body(): other = lax.ppermute(qkv[1:], 'seq', partner)  33.3 us
    all_to_all x1, blocking collectives, body(): x_clip = lax.all_to_all(x_parts, 'seq', 0, 0, tiled=True)  30.2 us
    pallas_call x1, Pallas kernels, project(): pl.pallas_call(kernel, grid=(3 * heads,), in_specs=[pl.BlockSpec((rows, w...  20.5 us
    pallas_call x1, Pallas kernels, attend(): pl.pallas_call(kernel, grid=(heads, rows // block_q), in_specs=[pl.BlockS...  19 us
    all_to_all x1, waiting for transfers between devices, body(): lax.all_to_all(branch_clip, 'seq', 0, 0, tiled=True)  18 us
  transfers between devices with their start and end apart: 5, of which 4 were waited for; matrix products, arithmetic and copies ran while one was open for 0% of the time, Pallas kernels for 0%

profile of v2, /device:TPU:1, one launch (start us, length us, event | category | flops | bytes accessed | tf_op | source)
XLA Modules:
  0.0 365.4 jit_solution(2003064144702379725)
XLA Ops:
  7.2 0.0 copy-start
  7.2 0.0 copy-start.4
  7.2 0.0 all-gather.3.cloned.1.call-start
  7.2 1.5 convert_reduce_fusion.1
  8.7 1.5 fusion.11
  10.3 0.1 div.15
  10.3 0.0 copy-done.4
  10.4 0.7 slice_bitcast_fusion.1
  11.1 0.1 add.63
  11.1 0.1 add.64
  11.3 1.0 mul.70
  12.3 0.8 mul.71
  13.1 0.1 rsqrt.20
  13.1 0.0 copy-done.1
  13.1 1.3 add_convert_fusion
  14.5 0.0 copy-start.6
  14.5 30.2 %all_to_all.10 = bf16[16,8,3072]{2,1,0:T(8,128)(2,1)} all-to-all(bf16[16,8,3072]{2,1,0:T(8,128)(2,1)S(1)} %add_convert_fusion), channel_id=1, replica_groups=mesh['comp'=2,'seq'=16,'tp'=8] {'seq'}, dimensions={0} | all-to-all | bytes 1572864 | tf_op jit(solution)/shard_map/all_to_all | solution.py:121
  44.7 0.0 all-gather.3.cloned.1.call-update
  44.7 0.0 reduce-scatter.2.cloned.1.call-start
  44.8 0.0 copy-done.6
  44.8 93.5 %all-gather.3.cloned.1.call-done = bf16[128,8,3072]{2,1,0:T(8,128)(2,1)} async-done(((bf16[16,8,3072]{2,1,0:T(8,128)(2,1)}), bf16[128,8,3072]{2,1,0:T(8,128)(2,1)}) %all-gather.3.cloned.1.call-update) | async-done | bytes 6291472 | tf_op jit(solution)/shard_map/all_gather | solution.py:122
  138.3 20.5 %shard_map.112.q_ref.k_ref.v_ref = bf16[3,1024,384]{2,1,0:T(8,128)(2,1)S(1)} custom-call(bf16[1024,3072]{1,0:T(8,128)(2,1)} %bitcast.63, bf16[3,3072,384]{2,1,0:T(8,128)(2,1)} %bitcast.61, f32[3,128]{1,0:T(4,128)S(1)} %concatenate.3.g_ref), custom_call_target="tpu_custom_call" | custom-call | tf_op jit(solution)/shard_map/pallas_call | solution.py:49
  158.8 0.2 slice.35
  159.0 1.4 collective-permute-start
  160.3 33.3 %collective-permute-done.ko_ref.vo_ref = bf16[2,1024,384]{2,1,0:T(8,128)(2,1)S(1)} collective-permute-done((bf16[2,1024,384]{2,1,0:T(8,128)(2,1)S(1)}, bf16[2,1024,384]{2,1,0:T(8,128)(2,1)S(1)}, u32[]{:S(2)}, u32[]{:S(2)}) %collective-permute-start) | collective-permute-done | bytes 1572896 | tf_op jit(solution)/shard_map/ppermute | solution.py:134
  193.6 19.0 %shard_map.113 = bf16[1024,384]{1,0:T(8,128)(2,1)S(1)} custom-call(bf16[3,1024,384]{2,1,0:T(8,128)(2,1)S(1)} %shard_map.112.q_ref.k_ref.v_ref, bf16[3,1024,384]{2,1,0:T(8,128)(2,1)S(1)} %shard_map.112.q_ref.k_ref.v_ref, bf16[3,1024,384]{2,1,0:T(8,128)(2,1)S(1)} %shard_map.112.q_ref.k_ref.v_ref, bf16[2,1024,384]{2,1,0:T(8,128)(2,1)S(1)} %collective-permute-done.ko_ref.vo_ref, ...), custom_call_target="tpu_custom_call" | custom-call | tf_op jit(solution)/shard_map/pallas_call | solution.py:92
  212.6 0.0 copy-done
  212.6 5.4 %convolution_convert_fusion = bf16[1024,3072]{1,0:T(8,128)(2,1)} fusion(bf16[1024,384]{1,0:T(8,128)(2,1)S(1)} %shard_map.113, bf16[1,384,3072]{2,1,0:T(8,128)(2,1)S(1)} %copy-done), kind=kOutput, calls=%fused_computation | convolution fusion | flops 2419064832 | bytes 9437184 | tf_op jit(solution)/shard_map/re,ed->rd/dot_general | solution.py:136
  218.0 0.0 reduce-scatter.2.cloned.1.call-update
  218.0 0.0 copy-start.5
  218.1 0.0 copy-start.2
  218.1 102.6 %reduce-scatter.2.cloned.1.call-done = bf16[1,128,3072]{2,1,0:T(8,128)(2,1)} async-done(((bf16[8,128,3072]{2,1,0:T(8,128)(2,1)}), bf16[1,128,3072]{2,1,0:T(8,128)(2,1)}) %reduce-scatter.2.cloned.1.call-update) | async-done | bytes 786448 | tf_op jit(solution)/shard_map/reduce_scatter | solution.py:139
  320.6 6.9 %all-to-all-start.1 = ((bf16[16,8,3072]{2,1,0:T(8,128)(2,1)}), bf16[16,8,3072]{2,1,0:T(8,128)(2,1)}, u32[]{:S(2)}, u32[]{:S(2)}) async-start(bf16[16,8,3072]{2,1,0:T(8,128)(2,1)} %bitcast.64), calls=%async_computation.2 | async-start | bytes 1572864 | tf_op jit(solution)/shard_map/all_to_all | solution.py:146
  327.6 0.0 copy-done.5
  327.6 0.2 fusion.20
  327.8 18.0 %all-to-all-done.1 = bf16[16,8,3072]{2,1,0:T(8,128)(2,1)} async-done(((bf16[16,8,3072]{2,1,0:T(8,128)(2,1)}), bf16[16,8,3072]{2,1,0:T(8,128)(2,1)}, u32[]{:S(2)}, u32[]{:S(2)}) %all-to-all-start.1) | async-done | bytes 786464 | tf_op jit(solution)/shard_map/all_to_all | solution.py:146
  345.8 1.5 convert_reduce_fusion
  347.3 0.0 copy-start.3
  347.3 0.3 fusion.4
  347.7 0.0 copy-done.8
  347.7 0.5 fusion.18
  348.2 0.1 copy-done.3
  348.3 1.2 fusion
  349.6 3.8 %collective-permute-start.1 = (bf16[8,16,3072]{2,1,0:T(8,128)(2,1)}, bf16[8,16,3072]{2,1,0:T(8,128)(2,1)S(1)}, u32[]{:S(2)}, u32[]{:S(2)}) collective-permute-start(bf16[8,16,3072]{2,1,0:T(8,128)(2,1)} %fusion), channel_id=1, source_target_pairs={{128,0},{0,128},{129,1},{1,129},{130,2},{2,130},{131,3},{3,131},{1... | collective-permute-start | bytes 2359304 | tf_op jit(solution)/shard_map/ppermute | solution.py:21
  353.4 3.6 psum.7
  357.0 0.7 slice_bitcast_fusion.2
  357.6 0.0 collective-permute-done.1
  357.6 0.9 copy.24
  (13 shorter events, 0.1 us)
Async XLA Ops:
  7.2 205.4 %copy-start = (bf16[1,384,3072]{2,1,0:T(8,128)(2,1)S(1)}, bf16[1,384,3072]{2,1,0:T(8,128)(2,1)}, u32[]{:S(2)}) copy-start(bf16[1,384,3072]{2,1,0:T(8,128)(2,1)} %param.12) | copy-start | bytes 7077892
  7.2 3.2 copy-start.4
  7.2 131.1 %all-gather.3.cloned.1.call-start = ((), (), s32[]{:S(2)}) async-start(), calls=%async_computation.4 | async-start | bytes 7077888 | tf_op jit(solution)/shard_map/all_gather | solution.py:122
  8.7 4.4 %copy-start.1 = (bf16[1,8,16,3072]{3,2,1,0:T(8,128)(2,1)S(1)}, bf16[1,8,16,3072]{3,2,1,0:T(8,128)(2,1)}, u32[]{:S(2)}) copy-start(bf16[1,8,16,3072]{3,2,1,0:T(8,128)(2,1)} %param.9) | copy-start | bytes 2359300
  14.5 30.3 %copy-start.6 = (f32[1,2,128]{2,1,0:T(2,128)S(1)}, f32[1,2,128]{2,1,0:T(2,128)}, u32[]{:S(2)}) copy-start(f32[1,2,128]{2,1,0:T(2,128)} %param.13) | copy-start | bytes 3076
  44.7 275.9 %reduce-scatter.2.cloned.1.call-start = ((), (), s32[]{:S(2)}) async-start(), calls=%async_computation.3 | async-start | bytes 7077888 | tf_op jit(solution)/shard_map/reduce_scatter | solution.py:139
  159.0 34.6 %collective-permute-start = (bf16[2,1024,384]{2,1,0:T(8,128)(2,1)S(1)}, bf16[2,1024,384]{2,1,0:T(8,128)(2,1)S(1)}, u32[]{:S(2)}, u32[]{:S(2)}) collective-permute-start(bf16[2,1024,384]{2,1,0:T(8,128)(2,1)S(1)} %slice.35), channel_id=1, source_target_pairs={{0,8},{8,0},{16,24},{24,16},{32,40},{40,32},{48,56},{56,48},{64,72... | collective-permute-start | bytes 4718600 | tf_op jit(solution)/shard_map/ppermute | solution.py:134
  218.0 109.5 %copy-start.5 = (f32[8,2,3072]{2,1,0:T(2,128)S(1)}, f32[8,2,3072]{2,1,0:T(2,128)}, u32[]{:S(2)}) copy-start(f32[8,2,3072]{2,1,0:T(2,128)} %param.14) | copy-start | bytes 589828
  218.1 127.7 %copy-start.2 = (f32[8,3072]{1,0:T(8,128)S(1)}, f32[8,3072]{1,0:T(8,128)}, u32[]{:S(2)}) copy-start(f32[8,3072]{1,0:T(8,128)} %get-tuple-element.5) | copy-start | bytes 294916
  320.6 25.1 %all-to-all-start.1 = ((bf16[16,8,3072]{2,1,0:T(8,128)(2,1)}), bf16[16,8,3072]{2,1,0:T(8,128)(2,1)}, u32[]{:S(2)}, u32[]{:S(2)}) async-start(bf16[16,8,3072]{2,1,0:T(8,128)(2,1)} %bitcast.64), calls=%async_computation.2 | async-start | bytes 1572864 | tf_op jit(solution)/shard_map/all_to_all | solution.py:146
  345.8 1.9 copy-start.7
  345.8 1.9 copy-start.8
  347.3 1.0 copy-start.3
  349.6 8.1 %collective-permute-start.1 = (bf16[8,16,3072]{2,1,0:T(8,128)(2,1)}, bf16[8,16,3072]{2,1,0:T(8,128)(2,1)S(1)}, u32[]{:S(2)}, u32[]{:S(2)}) collective-permute-start(bf16[8,16,3072]{2,1,0:T(8,128)(2,1)} %fusion), channel_id=1, source_target_pairs={{128,0},{0,128},{129,1},{1,129},{130,2},{2,130},{131,3},{3,131},{1... | collective-permute-start | bytes 2359304 | tf_op jit(solution)/shard_map/ppermute | solution.py:21
Sparse Core Ops, SparseCore 0:
  44.8 93.4 all-gather.2
  218.2 102.4 reduce-scatter.1

commit v3 on v2

v3 whole, which is shorter than its diff:
```python
import jax
import jax.numpy as jnp
from jax import lax
import functools
from jax.experimental import pallas as pl
from jax.experimental.pallas import tpu as pltpu
from jax.sharding import PartitionSpec as P

step_size = 0.02
norm_eps = 1e-06


def broadcast(block, axis, owner):
    block = jnp.where(lax.axis_index(axis) == owner, block, jnp.zeros_like(block))
    return lax.psum(block, axis)


def shifted(block, axis, distance):
    devices = range(lax.axis_size(axis))
    route = [((i - distance) % len(devices), i) for i in devices]
    return lax.ppermute(block, axis, route)


def layer_norm(values):
    center = values - jnp.mean(values, -1, keepdims=True)
    return center * lax.rsqrt(jnp.mean(center * center, -1, keepdims=True) + norm_eps)


def rms_norm(values, norm_gain):
    return values * lax.rsqrt(jnp.mean(values * values, -1, keepdims=True) + norm_eps) * norm_gain


def _project_kernel(x_ref, w_ref, g_ref, o_ref, *, heads, head_dim):
    which = pl.program_id(0)
    mixed = jnp.dot(x_ref[...], w_ref[...], preferred_element_type=jnp.float32)
    gain = g_ref[pl.ds(which, 1), :]
    for h in range(heads):
        block = mixed[:, h * head_dim : (h + 1) * head_dim]
        normed = (
            block * lax.rsqrt(jnp.mean(block * block, -1, keepdims=True) + norm_eps) * gain
        )
        o_ref[:, h * head_dim : (h + 1) * head_dim] = jnp.where(
            which < 2, normed, block
        ).astype(o_ref.dtype)


def project(x, w, gains, head_dim):
    rows, width = x.shape
    local_width = w.shape[2]
    heads = local_width // head_dim
    kernel = functools.partial(_project_kernel, heads=heads, head_dim=head_dim)
    return pl.pallas_call(
        kernel,
        grid=(3,),
        in_specs=[
            pl.BlockSpec((rows, width), lambda c: (0, 0)),
            pl.BlockSpec((None, width, local_width), lambda c: (c, 0, 0)),
            pl.BlockSpec(gains.shape, lambda c: (0, 0)),
        ],
        out_specs=pl.BlockSpec((None, rows, local_width), lambda c: (c, 0, 0)),
        out_shape=jax.ShapeDtypeStruct((3, rows, local_width), jnp.bfloat16),
        compiler_params=pltpu.CompilerParams(vmem_limit_bytes=48 * 1024 * 1024),
    )(x, w, gains)


def _attend_kernel(*refs, scaling, sources):
    q_ref, o_ref = refs[0], refs[-1]
    pairs = refs[1:-1]

    def scores_of(keys):
        return lax.dot_general(
            q_ref[...], keys[...], (((1,), (1,)), ((), ())), preferred_element_type=jnp.float32
        ) * scaling

    scores = [scores_of(pairs[2 * n]) for n in range(sources)]
    row_max = jnp.max(scores[0], -1, keepdims=True)
    for block in scores[1:]:
        row_max = jnp.maximum(row_max, jnp.max(block, -1, keepdims=True))
    weights = [jnp.exp(block - row_max) for block in scores]
    row_sum = sum(jnp.sum(block, -1, keepdims=True) for block in weights)
    summed = sum(
        jnp.dot(block.astype(jnp.bfloat16), pairs[2 * n + 1][...], preferred_element_type=jnp.float32)
        for n, block in enumerate(weights)
    )
    o_ref[...] = (summed / row_sum).astype(o_ref.dtype)


def attend(queries, key_sources, head_dim, block_q=512):
    rows, width = queries.shape[1], queries.shape[2]
    heads = width // head_dim
    block_q = min(block_q, rows)
    kernel = functools.partial(
        _attend_kernel, scaling=head_dim ** (-0.5), sources=len(key_sources)
    )
    in_specs = [pl.BlockSpec((None, block_q, head_dim), lambda h, i: (0, i, h))]
    operands = [queries]
    for source, first in key_sources:
        extent = source.shape[1]
        for index in (first, first + 1):
            in_specs.append(
                pl.BlockSpec((None, extent, head_dim), lambda h, i, index=index: (index, 0, h))
            )
            operands.append(source)
    return pl.pallas_call(
        kernel,
        grid=(heads, rows // block_q),
        in_specs=in_specs,
        out_specs=pl.BlockSpec((block_q, head_dim), lambda h, i: (i, h)),
        out_shape=jax.ShapeDtypeStruct((rows, width), jnp.bfloat16),
        compiler_params=pltpu.CompilerParams(vmem_limit_bytes=48 * 1024 * 1024),
    )(*operands)


def body(inputs, modulation, w_qkv, w_attn_out, qk_gain, final_mod, w_final, w_embed, latent):
    head_dim = qk_gain.shape[2]
    x_rows = inputs[0]
    samples, tokens_local, width = x_rows.shape
    n_seq = lax.axis_size("seq")
    parts = n_seq // samples
    part_tokens = tokens_local // parts
    mod_rows = modulation[0]
    x_float = x_rows.astype(jnp.float32)
    x_mod = (
        layer_norm(x_float) * (1.0 + mod_rows[:, 1, None, :]) + mod_rows[:, 0, None, :]
    ).astype(jnp.bfloat16)
    x_parts = x_mod.reshape(samples * parts, part_tokens, width)
    weights = jnp.transpose(w_qkv[0], (1, 0, 2))
    local_width = weights.shape[2]
    norm_gains = qk_gain[0]
    gains = jnp.concatenate([norm_gains, jnp.ones_like(norm_gains[:1])], 0)
    partner = [(i, i ^ 1) for i in range(n_seq)]
    chunks = 2
    chunk_tokens = part_tokens // chunks
    projected, others = [], []
    for c in range(chunks):
        x_clip = lax.all_to_all(
            x_parts[:, c * chunk_tokens : (c + 1) * chunk_tokens], "seq", 0, 0, tiled=True
        )
        x_group = lax.all_gather(x_clip, "tp", axis=0, tiled=False)
        n_tp, n_src = x_group.shape[0], x_group.shape[1]
        rows = n_tp * n_src * chunk_tokens
        qkv = project(x_group.reshape(rows, width), weights, gains, head_dim)
        projected.append(qkv)
        others.append(lax.ppermute(qkv[1:], "seq", partner))
    key_sources = [(qkv, 1) for qkv in projected] + [(other, 0) for other in others]
    pieces = []
    for c in range(chunks):
        attended = attend(projected[c], key_sources, head_dim)
        partial_out = jnp.einsum(
            "re,ed->rd", attended, w_attn_out[0], preferred_element_type=jnp.float32
        )
        branch_clip = lax.psum_scatter(
            partial_out.astype(jnp.bfloat16).reshape(n_tp, n_src * chunk_tokens, width),
            "tp",
            scatter_dimension=0,
            tiled=True,
        ).reshape(n_src, chunk_tokens, width)
        pieces.append(lax.all_to_all(branch_clip, "seq", 0, 0, tiled=True))
    branch = (
        jnp.stack(pieces, 1)
        .reshape(samples, tokens_local, width)
        .astype(jnp.float32)
    )
    output = (x_float + mod_rows[:, 2, None, :] * branch).astype(jnp.bfloat16)
    final_in = (
        layer_norm(output.astype(jnp.float32)) * (1.0 + final_mod[:, 1, None, :])
        + final_mod[:, 0, None, :]
    ).astype(jnp.bfloat16)
    velocity = jnp.einsum("srd,dc->scr", final_in, w_final, preferred_element_type=jnp.float32)
    advanced = latent + step_size * velocity
    last_comp = lax.axis_size("comp") - 1
    position = lax.axis_index("comp")
    shared = broadcast(
        jnp.stack([velocity, advanced]).astype(jnp.bfloat16), "comp", last_comp
    ).astype(jnp.float32)
    embedded = jnp.einsum(
        "scr,cd->srd", advanced.astype(jnp.bfloat16), w_embed, preferred_element_type=jnp.float32
    ).astype(jnp.bfloat16)
    sending = jnp.where(position == last_comp, embedded, output)
    handed = shifted(sending, "comp", 1)
    return (handed[None], shared[0], shared[1])


def solution(mesh):
    in_specs = (
        P("comp", None, ("seq", "tp"), None),
        P("comp", None, None, None),
        P("comp", None, None, "tp"),
        P("comp", "tp", None),
        P("comp", None, None),
        P(),
        P(),
        P(),
        P(None, None, ("seq", "tp")),
    )
    out_specs = (
        P("comp", None, ("seq", "tp"), None),
        P(None, None, ("seq", "tp")),
        P(None, None, ("seq", "tp")),
    )
    return jax.shard_map(body, mesh=mesh, in_specs=in_specs, out_specs=out_specs, check_vma=False)
```

time: 366 us -> 452 us (1.23)
  waiting for transfers between devices: 247 us -> 294 us
  local copies, waits for them, and re-layouts: 4.13 us -> 30.2 us
  blocking collectives: 33.8 us -> 41.7 us
  starting transfers between devices: 12.1 us -> 20 us
  Pallas kernels: 39.5 us -> 33.5 us
    reduce_scatter x1 -> x2, waiting for transfers between devices: 103 us -> 147 us  [body(): lax.psum_scatter(partial_out.astype(jnp.bfloat16).reshape(n_tp, n_src * c...]
    reshape x0 -> x4, local copies, waits for them, and re-layouts: none -> 15.6 us  [the longest x2 11.8 us: body(): qkv = project(x_group.reshape(rows, width), weights, gains, head_dim)]
    all_gather x1 -> x2, waiting for transfers between devices: 93.5 us -> 104 us  [body(): x_group = lax.all_gather(x_clip, 'tp', axis=0, tiled=False)]
    all_to_all x1 -> x2, waiting for transfers between devices: 18 us -> 8.99 us  [body(): pieces.append(lax.all_to_all(branch_clip, 'seq', 0, 0, tiled=True))]
    all_to_all x1 -> x2, blocking collectives: 30.2 us -> 38.1 us  [body(): lax.all_to_all(x_parts[:, c * chunk_tokens:(c + 1) * chunk_tokens], 'seq'...]
    unnamed x19 -> x37, local copies, waits for them, and re-layouts: 1.04 us -> 8.37 us
    all_to_all x1 -> x2, starting transfers between devices: 6.9 us -> 13.8 us  [body(): pieces.append(lax.all_to_all(branch_clip, 'seq', 0, 0, tiled=True))]
    pallas_call x2 -> x4, Pallas kernels: 39.5 us -> 33.5 us  [the longest x2 18.4 us: attend(): pl.pallas_call(kernel, grid=(heads, rows // block_q), in_specs=in_specs,...]
  transfers between devices with their start and end apart: 5 -> 9, of which waited for: 4 -> 7; matrix products, arithmetic and copies ran while one was open for 0% -> 3% of each run, Pallas kernels for 0% -> 4%
where the time goes in v3:
time: 452 us; the launch traced here: 451 us
  waiting for transfers between devices  294 us (65%)
  blocking collectives  41.7 us (9%)
  Pallas kernels  33.5 us (7%)
  local copies, waits for them, and re-layouts  30.2 us (7%)
  starting transfers between devices  20 us (4%)
  between operations  14.1 us (3%)
  other arithmetic  8.84 us (2%)
  matrix products  8.65 us (2%)
    reduce_scatter x2, waiting for transfers between devices, body(): lax.psum_scatter(partial_out.astype(jnp.bfloat16).reshape(n_tp, n_src * c...  147 us
    all_gather x2, waiting for transfers between devices, body(): x_group = lax.all_gather(x_clip, 'tp', axis=0, tiled=False)  104 us
    all_to_all x2, blocking collectives, body(): lax.all_to_all(x_parts[:, c * chunk_tokens:(c + 1) * chunk_tokens], 'seq'...  38.1 us
    ppermute x2, waiting for transfers between devices, body(): others.append(lax.ppermute(qkv[1:], 'seq', partner))  32.9 us
    pallas_call x2, Pallas kernels, attend(): pl.pallas_call(kernel, grid=(heads, rows // block_q), in_specs=in_specs,...  18.4 us
    pallas_call x2, Pallas kernels, project(): pl.pallas_call(kernel, grid=(3,), in_specs=[pl.BlockSpec((rows, width), l...  15.1 us
    all_to_all x2, starting transfers between devices, body(): pieces.append(lax.all_to_all(branch_clip, 'seq', 0, 0, tiled=True))  13.8 us
    reshape x2, local copies, waits for them, and re-layouts, body(): qkv = project(x_group.reshape(rows, width), weights, gains, head_dim)  11.8 us
  transfers between devices with their start and end apart: 9, of which 7 were waited for; matrix products, arithmetic and copies ran while one was open for 3% of the time, Pallas kernels for 4%

profile of v3, /device:TPU:1, one launch (start us, length us, event | category | flops | bytes accessed | tf_op | source)
XLA Modules:
  0.0 450.6 jit_solution(5214910378797156323)
XLA Ops:
  7.2 1.5 convert_reduce_fusion.1
  8.7 1.5 fusion.10
  10.4 0.7 slice_bitcast_fusion.1
  11.1 0.1 add.66
  11.3 1.0 mul.70
  12.3 0.8 mul.71
  13.1 1.3 add_convert_fusion
  14.5 0.3 fusion.20
  14.8 21.1 %all_to_all.20 = bf16[16,4,3072]{2,1,0:T(4,128)(2,1)} all-to-all(bf16[16,4,3072]{2,1,0:T(4,128)(2,1)S(1)} %get-tuple-element.6), channel_id=1, replica_groups=mesh['comp'=2,'seq'=16,'tp'=8] {'seq'}, dimensions={0} | all-to-all | bytes 786432 | tf_op jit(solution)/shard_map/all_to_all | solution.py:136
  35.9 17.1 %all_to_all.21 = bf16[16,4,3072]{2,1,0:T(4,128)(2,1)} all-to-all(bf16[16,4,3072]{2,1,0:T(4,128)(2,1)S(1)} %get-tuple-element.5), channel_id=1, replica_groups=mesh['comp'=2,'seq'=16,'tp'=8] {'seq'}, dimensions={0} | all-to-all | bytes 786432 | tf_op jit(solution)/shard_map/all_to_all | solution.py:136
  53.0 50.5 %all-gather.7.cloned.1.call-done = bf16[128,4,3072]{2,1,0:T(4,128)(2,1)} async-done(((bf16[16,4,3072]{2,1,0:T(4,128)(2,1)}), bf16[128,4,3072]{2,1,0:T(4,128)(2,1)}) %all-gather.7.cloned.1.call-update) | async-done | bytes 3145744 | tf_op jit(solution)/shard_map/all_gather | solution.py:139
  103.6 5.9 %reshape.72.x_ref = bf16[512,3072]{1,0:T(8,128)(2,1)} reshape(bf16[128,4,3072]{2,1,0:T(4,128)(2,1)} %all-gather.7.cloned.1.call-done) | data formatting | bytes 6291456 | tf_op jit(solution)/shard_map/reshape | solution.py:142
  109.5 1.9 copy-done.8
  111.3 7.5 %shard_map.113.refs_3_.refs_4_.refs_0_ = bf16[3,512,384]{2,1,0:T(8,128)(2,1)S(1)} custom-call(bf16[512,3072]{1,0:T(8,128)(2,1)S(1)} %copy-done.8, bf16[3,3072,384]{2,1,0:T(8,128)(2,1)} %bitcast.62, f32[3,128]{1,0:T(4,128)S(1)} %concatenate.3.g_ref), custom_call_target="tpu_custom_call" | custom-call | tf_op jit(solution)/shard_map/pallas_call | solution.py:52
  118.9 53.8 %all-gather.5.cloned.1.call-done = bf16[128,4,3072]{2,1,0:T(4,128)(2,1)} async-done(((bf16[16,4,3072]{2,1,0:T(4,128)(2,1)}), bf16[128,4,3072]{2,1,0:T(4,128)(2,1)}) %all-gather.5.cloned.1.call-update) | async-done | bytes 3145744 | tf_op jit(solution)/shard_map/all_gather | solution.py:139
  172.7 5.9 %reshape.71.x_ref = bf16[512,3072]{1,0:T(8,128)(2,1)} reshape(bf16[128,4,3072]{2,1,0:T(4,128)(2,1)} %all-gather.5.cloned.1.call-done) | data formatting | bytes 6291456 | tf_op jit(solution)/shard_map/reshape | solution.py:142
  178.6 1.9 copy-done.7
  180.5 7.5 %shard_map.112.refs_0_.refs_1_.refs_2_ = bf16[3,512,384]{2,1,0:T(8,128)(2,1)S(1)} custom-call(bf16[512,3072]{1,0:T(8,128)(2,1)S(1)} %copy-done.7, bf16[3,3072,384]{2,1,0:T(8,128)(2,1)} %bitcast.63, f32[3,128]{1,0:T(4,128)S(1)} %concatenate.3.g_ref), custom_call_target="tpu_custom_call" | custom-call | tf_op jit(solution)/shard_map/pallas_call | solution.py:52
  188.2 1.4 collective-permute-start
  189.6 0.3 collective-permute-start.1
  189.9 16.1 %collective-permute-done.refs_5_.refs_6_ = bf16[2,512,384]{2,1,0:T(8,128)(2,1)S(1)} collective-permute-done((bf16[2,512,384]{2,1,0:T(8,128)(2,1)S(1)}, bf16[2,512,384]{2,1,0:T(8,128)(2,1)S(1)}, u32[]{:S(2)}, u32[]{:S(2)}) %collective-permute-start) | collective-permute-done | bytes 786464 | tf_op jit(solution)/shard_map/ppermute | solution.py:144
  206.0 16.9 %collective-permute-done.1.refs_7_.refs_8_ = bf16[2,512,384]{2,1,0:T(8,128)(2,1)S(1)} collective-permute-done((bf16[2,512,384]{2,1,0:T(8,128)(2,1)S(1)}, bf16[2,512,384]{2,1,0:T(8,128)(2,1)S(1)}, u32[]{:S(2)}, u32[]{:S(2)}) %collective-permute-start.1) | collective-permute-done | bytes 786464 | tf_op jit(solution)/shard_map/ppermute | solution.py:144
  222.8 9.2 %shard_map.115 = bf16[512,384]{1,0:T(8,128)(2,1)S(1)} custom-call(bf16[3,512,384]{2,1,0:T(8,128)(2,1)S(1)} %shard_map.113.refs_3_.refs_4_.refs_0_, bf16[3,512,384]{2,1,0:T(8,128)(2,1)S(1)} %shard_map.112.refs_0_.refs_1_.refs_2_, bf16[3,512,384]{2,1,0:T(8,128)(2,1)S(1)} %shard_map.112.refs_0_.refs_1_.refs_2_, ...), custom_call_target="tpu_custom_call" | custom-call | tf_op jit(solution)/shard_map/pallas_call | solution.py:104
  232.0 3.4 convolution_convert_fusion
  235.5 0.2 reduce-scatter.3.cloned.1.call-start
  235.8 1.3 copy-done.2
  237.0 1.1 copy-done.4
  238.2 1.1 copy-done.6
  239.3 9.2 %shard_map.114 = bf16[512,384]{1,0:T(8,128)(2,1)S(1)} custom-call(bf16[3,512,384]{2,1,0:T(8,128)(2,1)S(1)} %copy-done.2, bf16[3,512,384]{2,1,0:T(8,128)(2,1)S(1)} %copy-done.2, bf16[3,512,384]{2,1,0:T(8,128)(2,1)S(1)} %copy-done.2, bf16[3,512,384]{2,1,0:T(8,128)(2,1)S(1)} %shard_map.113.refs_3_.refs_4_.refs_0_, ...), custom_call_target="tpu_custom_call" | custom-call | tf_op jit(solution)/shard_map/pallas_call | solution.py:104
  248.5 3.5 convolution_convert_fusion.1
  252.0 67.5 %reduce-scatter.5.cloned.1.call-done = bf16[1,64,3072]{2,1,0:T(8,128)(2,1)} async-done(((bf16[8,64,3072]{2,1,0:T(8,128)(2,1)}), bf16[1,64,3072]{2,1,0:T(8,128)(2,1)}) %reduce-scatter.5.cloned.1.call-update) | async-done | bytes 393232 | tf_op jit(solution)/shard_map/reduce_scatter | solution.py:152
  319.5 1.9 reshape.76
  321.4 6.9 %all-to-all-start.3 = ((bf16[16,4,3072]{2,1,0:T(4,128)(2,1)}), bf16[16,4,3072]{2,1,0:T(4,128)(2,1)S(1)}, u32[]{:S(2)}, u32[]{:S(2)}) async-start(bf16[16,4,3072]{2,1,0:T(4,128)(2,1)} %reshape.76), calls=%async_computation.5 | async-start | bytes 786432 | tf_op jit(solution)/shard_map/all_to_all | solution.py:158
  328.3 79.9 %reduce-scatter.3.cloned.1.call-done = bf16[1,64,3072]{2,1,0:T(8,128)(2,1)} async-done(((bf16[8,64,3072]{2,1,0:T(8,128)(2,1)}), bf16[1,64,3072]{2,1,0:T(8,128)(2,1)}) %reduce-scatter.3.cloned.1.call-update) | async-done | bytes 393232 | tf_op jit(solution)/shard_map/reduce_scatter | solution.py:152
  408.2 1.9 reshape.74
  410.1 6.9 %all-to-all-start.2 = ((bf16[16,4,3072]{2,1,0:T(4,128)(2,1)}), bf16[16,4,3072]{2,1,0:T(4,128)(2,1)S(1)}, u32[]{:S(2)}, u32[]{:S(2)}) async-start(bf16[16,4,3072]{2,1,0:T(4,128)(2,1)} %reshape.74), calls=%async_computation.3 | async-start | bytes 786432 | tf_op jit(solution)/shard_map/all_to_all | solution.py:158
  417.0 0.2 fusion.21
  417.2 9.0 %all-to-all-done.2 = bf16[16,4,3072]{2,1,0:T(4,128)(2,1)S(1)} async-done(((bf16[16,4,3072]{2,1,0:T(4,128)(2,1)}), bf16[16,4,3072]{2,1,0:T(4,128)(2,1)S(1)}, u32[]{:S(2)}, u32[]{:S(2)}) %all-to-all-start.2) | async-done | bytes 393248 | tf_op jit(solution)/shard_map/all_to_all | solution.py:158
  426.2 1.6 maximum_convert_fusion
  427.8 2.9 reshape.78
  430.7 1.8 convert_reduce_fusion
  432.4 0.3 fusion.5
  432.8 0.5 fusion.18
  433.4 1.2 fusion
  434.7 4.3 collective-permute-start.2
  438.9 3.6 psum.7
  442.6 0.7 slice_bitcast_fusion.2
  443.2 0.9 copy.24
  (53 shorter events, 0.9 us)
Async XLA Ops:
  7.2 224.9 %copy-start = (bf16[1,384,3072]{2,1,0:T(8,128)(2,1)S(1)}, bf16[1,384,3072]{2,1,0:T(8,128)(2,1)}, u32[]{:S(2)}) copy-start(bf16[1,384,3072]{2,1,0:T(8,128)(2,1)} %param.12) | copy-start | bytes 7077892
  7.2 3.2 copy-start.13
  7.2 96.4 %all-gather.7.cloned.1.call-start = ((), (), s32[]{:S(2)}) async-start(), calls=%async_computation.9 | async-start | bytes 3538944 | tf_op jit(solution)/shard_map/all_gather | solution.py:139
  8.7 4.4 copy-start.9
  14.7 38.3 %copy-start.15 = (f32[1,2,128]{2,1,0:T(2,128)S(1)}, f32[1,2,128]{2,1,0:T(2,128)}, u32[]{:S(2)}) copy-start(f32[1,2,128]{2,1,0:T(2,128)} %param.13) | copy-start | bytes 3076
  35.8 136.9 %all-gather.5.cloned.1.call-start = ((), (), s32[]{:S(2)}) async-start(), calls=%async_computation.8 | async-start | bytes 3538944 | tf_op jit(solution)/shard_map/all_gather | solution.py:139
  53.0 266.5 %reduce-scatter.5.cloned.1.call-start = ((), (), s32[]{:S(2)}) async-start(), calls=%async_computation.7 | async-start | bytes 3538944 | tf_op jit(solution)/shard_map/reduce_scatter | solution.py:152
  109.5 1.9 copy-start.8
  178.6 1.9 copy-start.7
  188.1 34.7 %copy-start.1 = (bf16[3,512,384]{2,1,0:T(8,128)(2,1)}, bf16[3,512,384]{2,1,0:T(8,128)(2,1)S(1)}, u32[]{:S(2)}) copy-start(bf16[3,512,384]{2,1,0:T(8,128)(2,1)S(1)} %shard_map.112.refs_0_.refs_1_.refs_2_) | copy-start | bytes 3538948
  188.2 17.8 %collective-permute-start = (bf16[2,512,384]{2,1,0:T(8,128)(2,1)S(1)}, bf16[2,512,384]{2,1,0:T(8,128)(2,1)S(1)}, u32[]{:S(2)}, u32[]{:S(2)}) collective-permute-start(bf16[2,512,384]{2,1,0:T(8,128)(2,1)S(1)} %slice.49), channel_id=1, source_target_pairs={{0,8},{8,0},{16,24},{24,16},{32,40},{40,32},{48,56},{56,48},{64,72... | collective-permute-start | bytes 2359304 | tf_op jit(solution)/shard_map/ppermute | solution.py:144
  189.6 33.2 %collective-permute-start.1 = (bf16[2,512,384]{2,1,0:T(8,128)(2,1)S(1)}, bf16[2,512,384]{2,1,0:T(8,128)(2,1)S(1)}, u32[]{:S(2)}, u32[]{:S(2)}) collective-permute-start(bf16[2,512,384]{2,1,0:T(8,128)(2,1)S(1)} %slice.50), channel_id=1, source_target_pairs={{0,8},{8,0},{16,24},{24,16},{32,40},{40,32},{48,56},{56,48},{64,72... | collective-permute-start | bytes 2359304 | tf_op jit(solution)/shard_map/ppermute | solution.py:144
  205.9 26.1 %copy-start.3 = (bf16[2,512,384]{2,1,0:T(8,128)(2,1)}, bf16[2,512,384]{2,1,0:T(8,128)(2,1)S(1)}, u32[]{:S(2)}) copy-start(bf16[2,512,384]{2,1,0:T(8,128)(2,1)S(1)} %collective-permute-done.refs_5_.refs_6_) | copy-start | bytes 2359300
  222.8 9.2 %copy-start.5 = (bf16[2,512,384]{2,1,0:T(8,128)(2,1)}, bf16[2,512,384]{2,1,0:T(8,128)(2,1)S(1)}, u32[]{:S(2)}) copy-start(bf16[2,512,384]{2,1,0:T(8,128)(2,1)S(1)} %collective-permute-done.1.refs_7_.refs_8_) | copy-start | bytes 2359300
  235.5 172.7 %reduce-scatter.3.cloned.1.call-start = ((), (), s32[]{:S(2)}) async-start(), calls=%async_computation.6 | async-start | bytes 3538944 | tf_op jit(solution)/shard_map/reduce_scatter | solution.py:152
  235.7 1.3 copy-start.2
  237.0 1.1 copy-start.4
  238.2 1.1 copy-start.6
  252.0 165.0 %copy-start.14 = (f32[8,2,3072]{2,1,0:T(2,128)S(1)}, f32[8,2,3072]{2,1,0:T(2,128)}, u32[]{:S(2)}) copy-start(f32[8,2,3072]{2,1,0:T(2,128)} %param.14) | copy-start | bytes 589828
  321.4 88.7 %all-to-all-start.3 = ((bf16[16,4,3072]{2,1,0:T(4,128)(2,1)}), bf16[16,4,3072]{2,1,0:T(4,128)(2,1)S(1)}, u32[]{:S(2)}, u32[]{:S(2)}) async-start(bf16[16,4,3072]{2,1,0:T(4,128)(2,1)} %reshape.76), calls=%async_computation.5 | async-start | bytes 786432 | tf_op jit(solution)/shard_map/all_to_all | solution.py:158
  410.1 16.1 %all-to-all-start.2 = ((bf16[16,4,3072]{2,1,0:T(4,128)(2,1)}), bf16[16,4,3072]{2,1,0:T(4,128)(2,1)S(1)}, u32[]{:S(2)}, u32[]{:S(2)}) async-start(bf16[16,4,3072]{2,1,0:T(4,128)(2,1)} %reshape.74), calls=%async_computation.3 | async-start | bytes 786432 | tf_op jit(solution)/shard_map/all_to_all | solution.py:158
  427.8 2.9 copy-start.10
  427.8 2.9 copy-start.11
  430.6 2.1 copy-start.16
  430.7 2.2 copy-start.17
  432.4 1.0 copy-start.12
  434.7 8.6 %collective-permute-start.2 = (bf16[8,16,3072]{2,1,0:T(8,128)(2,1)}, bf16[8,16,3072]{2,1,0:T(8,128)(2,1)S(1)}, u32[]{:S(2)}, u32[]{:S(2)}) collective-permute-start(bf16[8,16,3072]{2,1,0:T(8,128)(2,1)} %fusion), channel_id=1, source_target_pairs={{128,0},{0,128},{129,1},{1,129},{130,2},{2,130},{131,3},{3,131},{1... | collective-permute-start | bytes 2359304 | tf_op jit(solution)/shard_map/ppermute | solution.py:21
Sparse Core Ops, SparseCore 0:
  36.0 67.5 all-gather.6
  106.2 66.5 all-gather.4
  235.6 83.7 reduce-scatter.4
  323.5 84.6 reduce-scatter.2

commit v4 on v3

--- a/solution.py
+++ b/solution.py
@@ -30,8 +30,8 @@
     return values * lax.rsqrt(jnp.mean(values * values, -1, keepdims=True) + norm_eps) * norm_gain
 
 
-def _project_kernel(x_ref, w_ref, g_ref, o_ref, *, heads, head_dim):
-    which = pl.program_id(0)
+def _project_kernel(x_ref, w_ref, g_ref, o_ref, *, heads, head_dim, first):
+    which = pl.program_id(0) + first
     mixed = jnp.dot(x_ref[...], w_ref[...], preferred_element_type=jnp.float32)
     gain = g_ref[pl.ds(which, 1), :]
     for h in range(heads):
@@ -44,21 +44,21 @@
         ).astype(o_ref.dtype)
 
 
-def project(x, w, gains, head_dim):
+def project(x, w, gains, head_dim, first, count):
     rows, width = x.shape
     local_width = w.shape[2]
     heads = local_width // head_dim
-    kernel = functools.partial(_project_kernel, heads=heads, head_dim=head_dim)
+    kernel = functools.partial(_project_kernel, heads=heads, head_dim=head_dim, first=first)
     return pl.pallas_call(
         kernel,
-        grid=(3,),
+        grid=(count,),
         in_specs=[
             pl.BlockSpec((rows, width), lambda c: (0, 0)),
-            pl.BlockSpec((None, width, local_width), lambda c: (c, 0, 0)),
+            pl.BlockSpec((None, width, local_width), lambda c: (c + first, 0, 0)),
             pl.BlockSpec(gains.shape, lambda c: (0, 0)),
         ],
         out_specs=pl.BlockSpec((None, rows, local_width), lambda c: (c, 0, 0)),
-        out_shape=jax.ShapeDtypeStruct((3, rows, local_width), jnp.bfloat16),
+        out_shape=jax.ShapeDtypeStruct((count, rows, local_width), jnp.bfloat16),
         compiler_params=pltpu.CompilerParams(vmem_limit_bytes=48 * 1024 * 1024),
     )(x, w, gains)
 
@@ -129,35 +129,26 @@
     norm_gains = qk_gain[0]
     gains = jnp.concatenate([norm_gains, jnp.ones_like(norm_gains[:1])], 0)
     partner = [(i, i ^ 1) for i in range(n_seq)]
-    chunks = 2
-    chunk_tokens = part_tokens // chunks
-    projected, others = [], []
-    for c in range(chunks):
-        x_clip = lax.all_to_all(
-            x_parts[:, c * chunk_tokens : (c + 1) * chunk_tokens], "seq", 0, 0, tiled=True
-        )
-        x_group = lax.all_gather(x_clip, "tp", axis=0, tiled=False)
-        n_tp, n_src = x_group.shape[0], x_group.shape[1]
-        rows = n_tp * n_src * chunk_tokens
-        qkv = project(x_group.reshape(rows, width), weights, gains, head_dim)
-        projected.append(qkv)
-        others.append(lax.ppermute(qkv[1:], "seq", partner))
-    key_sources = [(qkv, 1) for qkv in projected] + [(other, 0) for other in others]
-    pieces = []
-    for c in range(chunks):
-        attended = attend(projected[c], key_sources, head_dim)
-        partial_out = jnp.einsum(
-            "re,ed->rd", attended, w_attn_out[0], preferred_element_type=jnp.float32
-        )
-        branch_clip = lax.psum_scatter(
-            partial_out.astype(jnp.bfloat16).reshape(n_tp, n_src * chunk_tokens, width),
-            "tp",
-            scatter_dimension=0,
-            tiled=True,
-        ).reshape(n_src, chunk_tokens, width)
-        pieces.append(lax.all_to_all(branch_clip, "seq", 0, 0, tiled=True))
+    x_clip = lax.all_to_all(x_parts, "seq", 0, 0, tiled=True)
+    x_group = lax.all_gather(x_clip, "tp", axis=0, tiled=False)
+    n_tp, n_src = x_group.shape[0], x_group.shape[1]
+    rows = n_tp * n_src * part_tokens
+    x_group = x_group.reshape(rows, width)
+    pairs = project(x_group, weights, gains, head_dim, 1, 2)
+    other = lax.ppermute(pairs, "seq", partner)
+    queried = project(x_group, weights, gains, head_dim, 0, 1)
+    attended = attend(queried, [(pairs, 0), (other, 0)], head_dim)
+    partial_out = jnp.einsum(
+        "re,ed->rd", attended, w_attn_out[0], preferred_element_type=jnp.float32
+    )
+    branch_clip = lax.psum_scatter(
+        partial_out.astype(jnp.bfloat16).reshape(n_tp, n_src * part_tokens, width),
+        "tp",
+        scatter_dimension=0,
+        tiled=True,
+    ).reshape(n_src, part_tokens, width)
     branch = (
-        jnp.stack(pieces, 1)
+        lax.all_to_all(branch_clip, "seq", 0, 0, tiled=True)
         .reshape(samples, tokens_local, width)
         .astype(jnp.float32)
     )

time: 452 us -> 356 us (0.79)
  waiting for transfers between devices: 294 us -> 240 us
  local copies, waits for them, and re-layouts: 30.2 us -> 3.98 us
  blocking collectives: 41.7 us -> 33.8 us
  starting transfers between devices: 20 us -> 12.1 us
    reduce_scatter x2 -> x1, waiting for transfers between devices: 147 us -> 103 us  [body(): lax.psum_scatter(partial_out.astype(jnp.bfloat16).reshape(n_tp, n_src * p...]
    reshape x4 -> x0, local copies, waits for them, and re-layouts: 15.6 us -> none  [the longest x2 11.8 us: body(): qkv = project(x_group.reshape(rows, width), weights, gains, head_dim)]
    all_gather x2 -> x1, waiting for transfers between devices: 104 us -> 93.5 us  [body(): x_group = lax.all_gather(x_clip, 'tp', axis=0, tiled=False)]
    all_to_all x2 -> x1, waiting for transfers between devices: 8.99 us -> 18 us  [body(): lax.all_to_all(branch_clip, 'seq', 0, 0, tiled=True)]
    all_to_all x2 -> x1, blocking collectives: 38.1 us -> 30.2 us  [body(): x_clip = lax.all_to_all(x_parts, 'seq', 0, 0, tiled=True)]
    unnamed x37 -> x19, local copies, waits for them, and re-layouts: 8.37 us -> 1.04 us
    all_to_all x2 -> x1, starting transfers between devices: 13.8 us -> 6.93 us  [body(): lax.all_to_all(branch_clip, 'seq', 0, 0, tiled=True)]
    ppermute x2 -> x1, waiting for transfers between devices: 32.9 us -> 26.2 us  [body(): other = lax.ppermute(pairs, 'seq', partner)]
  transfers between devices with their start and end apart: 9 -> 5, of which waited for: 7 -> 4; matrix products, arithmetic and copies ran while one was open for 3% -> 0% of each run, Pallas kernels for 4% -> 2%
where the time goes in v4:
time: 356 us; the launch traced here: 355 us
  waiting for transfers between devices  240 us (67%)
  Pallas kernels  36.9 us (10%)
  blocking collectives  33.8 us (9%)
  between operations  14.3 us (4%)
  starting transfers between devices  12.1 us (3%)
  matrix products  7.15 us (2%)
  other arithmetic  7.02 us (2%)
  local copies, waits for them, and re-layouts  3.98 us (1%)
    reduce_scatter x1, waiting for transfers between devices, body(): lax.psum_scatter(partial_out.astype(jnp.bfloat16).reshape(n_tp, n_src * p...  103 us
    all_gather x1, waiting for transfers between devices, body(): x_group = lax.all_gather(x_clip, 'tp', axis=0, tiled=False)  93.5 us
    all_to_all x1, blocking collectives, body(): x_clip = lax.all_to_all(x_parts, 'seq', 0, 0, tiled=True)  30.2 us
    ppermute x1, waiting for transfers between devices, body(): other = lax.ppermute(pairs, 'seq', partner)  26.2 us
    pallas_call x1, Pallas kernels, attend(): pl.pallas_call(kernel, grid=(heads, rows // block_q), in_specs=in_specs,...  19 us
    all_to_all x1, waiting for transfers between devices, body(): lax.all_to_all(branch_clip, 'seq', 0, 0, tiled=True)  18 us
    pallas_call x2, Pallas kernels, project(): pl.pallas_call(kernel, grid=(count,), in_specs=[pl.BlockSpec((rows, width...  17.9 us
  transfers between devices with their start and end apart: 5, of which 4 were waited for; matrix products, arithmetic and copies ran while one was open for 0% of the time, Pallas kernels for 2%

profile of v4, /device:TPU:1, one launch (start us, length us, event | category | flops | bytes accessed | tf_op | source)
XLA Modules:
  0.0 355.4 jit_solution(4241626467206177365)
XLA Ops:
  7.2 0.0 copy-start
  7.2 0.0 copy-start.4
  7.2 0.0 all-gather.3.cloned.1.call-start
  7.2 1.5 convert_reduce_fusion.1
  8.7 1.5 fusion.11
  10.3 0.1 div.15
  10.3 0.0 copy-done.4
  10.4 0.7 slice_bitcast_fusion.1
  11.1 0.1 add.63
  11.1 0.1 add.64
  11.3 1.0 mul.70
  12.3 0.8 mul.71
  13.1 0.1 rsqrt.20
  13.1 0.0 copy-done.1
  13.1 1.3 add_convert_fusion
  14.5 0.0 copy-start.6
  14.5 30.2 %all_to_all.10 = bf16[16,8,3072]{2,1,0:T(8,128)(2,1)} all-to-all(bf16[16,8,3072]{2,1,0:T(8,128)(2,1)S(1)} %add_convert_fusion), channel_id=1, replica_groups=mesh['comp'=2,'seq'=16,'tp'=8] {'seq'}, dimensions={0} | all-to-all | bytes 1572864 | tf_op jit(solution)/shard_map/all_to_all | solution.py:132
  44.7 0.0 all-gather.3.cloned.1.call-update
  44.7 0.0 reduce-scatter.2.cloned.1.call-start
  44.8 0.0 copy-done.6
  44.8 93.5 %all-gather.3.cloned.1.call-done = bf16[128,8,3072]{2,1,0:T(8,128)(2,1)} async-done(((bf16[16,8,3072]{2,1,0:T(8,128)(2,1)}), bf16[128,8,3072]{2,1,0:T(8,128)(2,1)}) %all-gather.3.cloned.1.call-update) | async-done | bytes 6291472 | tf_op jit(solution)/shard_map/all_gather | solution.py:133
  138.3 10.8 %shard_map.113.refs_1_.refs_2_ = bf16[2,1024,384]{2,1,0:T(8,128)(2,1)S(1)} custom-call(bf16[1024,3072]{1,0:T(8,128)(2,1)} %bitcast.62, bf16[3,3072,384]{2,1,0:T(8,128)(2,1)} %bitcast.60, f32[3,128]{1,0:T(4,128)S(1)} %concatenate.3.g_ref), custom_call_target="tpu_custom_call" | custom-call | tf_op jit(solution)/shard_map/pallas_call | solution.py:52
  149.1 1.4 collective-permute-start
  150.5 7.1 %shard_map.112.refs_0_ = bf16[1,1024,384]{2,1,0:T(8,128)(2,1)S(1)} custom-call(bf16[1024,3072]{1,0:T(8,128)(2,1)} %bitcast.63, bf16[3,3072,384]{2,1,0:T(8,128)(2,1)} %bitcast.61, f32[3,128]{1,0:T(4,128)S(1)} %concatenate.3.g_ref), custom_call_target="tpu_custom_call" | custom-call | tf_op jit(solution)/shard_map/pallas_call | solution.py:52
  157.6 26.2 %collective-permute-done.refs_3_.refs_4_ = bf16[2,1024,384]{2,1,0:T(8,128)(2,1)S(1)} collective-permute-done((bf16[2,1024,384]{2,1,0:T(8,128)(2,1)S(1)}, bf16[2,1024,384]{2,1,0:T(8,128)(2,1)S(1)}, u32[]{:S(2)}, u32[]{:S(2)}) %collective-permute-start) | collective-permute-done | bytes 1572896 | tf_op jit(solution)/shard_map/ppermute | solution.py:138
  183.7 19.0 %shard_map.114 = bf16[1024,384]{1,0:T(8,128)(2,1)S(1)} custom-call(bf16[1,1024,384]{2,1,0:T(8,128)(2,1)S(1)} %shard_map.112.refs_0_, bf16[2,1024,384]{2,1,0:T(8,128)(2,1)S(1)} %shard_map.113.refs_1_.refs_2_, bf16[2,1024,384]{2,1,0:T(8,128)(2,1)S(1)} %shard_map.113.refs_1_.refs_2_, bf16[2,1024,384]{2,1,0:T(8,128)(2,1)S(1)} %collective-permute-done.refs_3_.refs_4_, ...), custom_call_target="tpu_custom_call" | custom-call | tf_op jit(solution)/shard_map/pallas_call | solution.py:104
  202.7 0.0 copy-done
  202.7 5.4 %convolution_convert_fusion = bf16[1024,3072]{1,0:T(8,128)(2,1)} fusion(bf16[1024,384]{1,0:T(8,128)(2,1)S(1)} %shard_map.114, bf16[1,384,3072]{2,1,0:T(8,128)(2,1)S(1)} %copy-done), kind=kOutput, calls=%fused_computation | convolution fusion | flops 2419064832 | bytes 9437184 | tf_op jit(solution)/shard_map/re,ed->rd/dot_general | solution.py:141
  208.2 0.0 reduce-scatter.2.cloned.1.call-update
  208.2 0.0 copy-start.5
  208.2 0.0 copy-start.2
  208.2 102.5 %reduce-scatter.2.cloned.1.call-done = bf16[1,128,3072]{2,1,0:T(8,128)(2,1)} async-done(((bf16[8,128,3072]{2,1,0:T(8,128)(2,1)}), bf16[1,128,3072]{2,1,0:T(8,128)(2,1)}) %reduce-scatter.2.cloned.1.call-update) | async-done | bytes 786448 | tf_op jit(solution)/shard_map/reduce_scatter | solution.py:144
  310.8 6.9 %all-to-all-start.1 = ((bf16[16,8,3072]{2,1,0:T(8,128)(2,1)}), bf16[16,8,3072]{2,1,0:T(8,128)(2,1)}, u32[]{:S(2)}, u32[]{:S(2)}) async-start(bf16[16,8,3072]{2,1,0:T(8,128)(2,1)} %bitcast.66), calls=%async_computation.2 | async-start | bytes 1572864 | tf_op jit(solution)/shard_map/all_to_all | solution.py:151
  317.7 0.0 copy-done.5
  317.7 0.2 fusion.20
  317.9 18.0 %all-to-all-done.1 = bf16[16,8,3072]{2,1,0:T(8,128)(2,1)} async-done(((bf16[16,8,3072]{2,1,0:T(8,128)(2,1)}), bf16[16,8,3072]{2,1,0:T(8,128)(2,1)}, u32[]{:S(2)}, u32[]{:S(2)}) %all-to-all-start.1) | async-done | bytes 786464 | tf_op jit(solution)/shard_map/all_to_all | solution.py:151
  335.9 1.5 convert_reduce_fusion
  337.4 0.0 copy-start.3
  337.4 0.3 fusion.4
  337.8 0.0 copy-done.8
  337.8 0.5 fusion.18
  338.3 0.1 copy-done.3
  338.4 1.2 fusion
  339.7 3.7 %collective-permute-start.1 = (bf16[8,16,3072]{2,1,0:T(8,128)(2,1)}, bf16[8,16,3072]{2,1,0:T(8,128)(2,1)S(1)}, u32[]{:S(2)}, u32[]{:S(2)}) collective-permute-start(bf16[8,16,3072]{2,1,0:T(8,128)(2,1)} %fusion), channel_id=1, source_target_pairs={{128,0},{0,128},{129,1},{1,129},{130,2},{2,130},{131,3},{3,131},{1... | collective-permute-start | bytes 2359304 | tf_op jit(solution)/shard_map/ppermute | solution.py:21
  343.4 3.6 %psum.7 = bf16[2,8,64,16]{2,3,1,0:T(8,128)(2,1)S(1)} all-reduce(bf16[2,8,64,16]{2,3,1,0:T(8,128)(2,1)S(1)} %maximum_select_fusion), channel_id=1, replica_groups=mesh['comp'=2,'seq'=16,'tp'=8] {'comp'}, use_global_device_ids=true, to_apply=%region_5.6 | all-reduce | flops 16384 | bytes 65536 | tf_op jit(solution)/shard_map/psum | solution.py:15
  347.0 0.7 slice_bitcast_fusion.2
  347.7 0.0 collective-permute-done.1
  347.7 0.9 copy.24
  (13 shorter events, 0.1 us)
Async XLA Ops:
  7.2 195.6 %copy-start = (bf16[1,384,3072]{2,1,0:T(8,128)(2,1)S(1)}, bf16[1,384,3072]{2,1,0:T(8,128)(2,1)}, u32[]{:S(2)}) copy-start(bf16[1,384,3072]{2,1,0:T(8,128)(2,1)} %param.12) | copy-start | bytes 7077892
  7.2 3.2 copy-start.4
  7.2 131.1 %all-gather.3.cloned.1.call-start = ((), (), s32[]{:S(2)}) async-start(), calls=%async_computation.4 | async-start | bytes 7077888 | tf_op jit(solution)/shard_map/all_gather | solution.py:133
  8.7 4.4 %copy-start.1 = (bf16[1,8,16,3072]{3,2,1,0:T(8,128)(2,1)S(1)}, bf16[1,8,16,3072]{3,2,1,0:T(8,128)(2,1)}, u32[]{:S(2)}) copy-start(bf16[1,8,16,3072]{3,2,1,0:T(8,128)(2,1)} %param.9) | copy-start | bytes 2359300
  14.5 30.3 %copy-start.6 = (f32[1,2,128]{2,1,0:T(2,128)S(1)}, f32[1,2,128]{2,1,0:T(2,128)}, u32[]{:S(2)}) copy-start(f32[1,2,128]{2,1,0:T(2,128)} %param.13) | copy-start | bytes 3076
  44.7 266.0 %reduce-scatter.2.cloned.1.call-start = ((), (), s32[]{:S(2)}) async-start(), calls=%async_computation.3 | async-start | bytes 7077888 | tf_op jit(solution)/shard_map/reduce_scatter | solution.py:144
  149.1 34.6 %collective-permute-start = (bf16[2,1024,384]{2,1,0:T(8,128)(2,1)S(1)}, bf16[2,1024,384]{2,1,0:T(8,128)(2,1)S(1)}, u32[]{:S(2)}, u32[]{:S(2)}) collective-permute-start(bf16[2,1024,384]{2,1,0:T(8,128)(2,1)S(1)} %shard_map.113.refs_1_.refs_2_), channel_id=1, source_target_pairs={{0,8},{8,0},{16,24},{24,16},{32,40},{40,32},{48,56},{56,48},{64,72... | collective-permute-start | bytes 4718600 | tf_op jit(solution)/shard_map/ppermute | solution.py:138
  208.2 109.5 %copy-start.5 = (f32[8,2,3072]{2,1,0:T(2,128)S(1)}, f32[8,2,3072]{2,1,0:T(2,128)}, u32[]{:S(2)}) copy-start(f32[8,2,3072]{2,1,0:T(2,128)} %param.14) | copy-start | bytes 589828
  208.2 127.7 %copy-start.2 = (f32[8,3072]{1,0:T(8,128)S(1)}, f32[8,3072]{1,0:T(8,128)}, u32[]{:S(2)}) copy-start(f32[8,3072]{1,0:T(8,128)} %get-tuple-element.5) | copy-start | bytes 294916
  310.8 25.1 %all-to-all-start.1 = ((bf16[16,8,3072]{2,1,0:T(8,128)(2,1)}), bf16[16,8,3072]{2,1,0:T(8,128)(2,1)}, u32[]{:S(2)}, u32[]{:S(2)}) async-start(bf16[16,8,3072]{2,1,0:T(8,128)(2,1)} %bitcast.66), calls=%async_computation.2 | async-start | bytes 1572864 | tf_op jit(solution)/shard_map/all_to_all | solution.py:151
  335.9 1.9 copy-start.7
  335.9 1.9 copy-start.8
  337.4 1.0 copy-start.3
  339.7 8.0 %collective-permute-start.1 = (bf16[8,16,3072]{2,1,0:T(8,128)(2,1)}, bf16[8,16,3072]{2,1,0:T(8,128)(2,1)S(1)}, u32[]{:S(2)}, u32[]{:S(2)}) collective-permute-start(bf16[8,16,3072]{2,1,0:T(8,128)(2,1)} %fusion), channel_id=1, source_target_pairs={{128,0},{0,128},{129,1},{1,129},{130,2},{2,130},{131,3},{3,131},{1... | collective-permute-start | bytes 2359304 | tf_op jit(solution)/shard_map/ppermute | solution.py:21
Sparse Core Ops, SparseCore 0:
  44.8 93.4 all-gather.2
  208.3 102.4 reduce-scatter.1

commit v5 on v4

--- a/solution.py
+++ b/solution.py
@@ -117,22 +117,22 @@
     samples, tokens_local, width = x_rows.shape
     n_seq = lax.axis_size("seq")
     parts = n_seq // samples
-    part_tokens = tokens_local // parts
     mod_rows = modulation[0]
     x_float = x_rows.astype(jnp.float32)
     x_mod = (
         layer_norm(x_float) * (1.0 + mod_rows[:, 1, None, :]) + mod_rows[:, 0, None, :]
     ).astype(jnp.bfloat16)
-    x_parts = x_mod.reshape(samples * parts, part_tokens, width)
     weights = jnp.transpose(w_qkv[0], (1, 0, 2))
     local_width = weights.shape[2]
     norm_gains = qk_gain[0]
     gains = jnp.concatenate([norm_gains, jnp.ones_like(norm_gains[:1])], 0)
-    partner = [(i, i ^ 1) for i in range(n_seq)]
-    x_clip = lax.all_to_all(x_parts, "seq", 0, 0, tiled=True)
+    ring = n_seq // parts
+    groups = [list(range(p * ring, (p + 1) * ring)) for p in range(parts)]
+    partner = [(i, (i + ring) % n_seq) for i in range(n_seq)]
+    x_clip = lax.all_to_all(x_mod, "seq", 0, 0, tiled=True, axis_index_groups=groups)
     x_group = lax.all_gather(x_clip, "tp", axis=0, tiled=False)
     n_tp, n_src = x_group.shape[0], x_group.shape[1]
-    rows = n_tp * n_src * part_tokens
+    rows = n_tp * n_src * tokens_local
     x_group = x_group.reshape(rows, width)
     pairs = project(x_group, weights, gains, head_dim, 1, 2)
     other = lax.ppermute(pairs, "seq", partner)
@@ -142,13 +142,13 @@
         "re,ed->rd", attended, w_attn_out[0], preferred_element_type=jnp.float32
     )
     branch_clip = lax.psum_scatter(
-        partial_out.astype(jnp.bfloat16).reshape(n_tp, n_src * part_tokens, width),
+        partial_out.astype(jnp.bfloat16).reshape(n_tp, n_src * tokens_local, width),
         "tp",
         scatter_dimension=0,
         tiled=True,
-    ).reshape(n_src, part_tokens, width)
+    ).reshape(n_src, tokens_local, width)
     branch = (
-        lax.all_to_all(branch_clip, "seq", 0, 0, tiled=True)
+        lax.all_to_all(branch_clip, "seq", 0, 0, tiled=True, axis_index_groups=groups)
         .reshape(samples, tokens_local, width)
         .astype(jnp.float32)
     )

time: 356 us -> 352 us (0.989)
    all_to_all x1, waiting for transfers between devices: 18 us -> 22.2 us  [body(): lax.all_to_all(branch_clip, 'seq', 0, 0, tiled=True, axis_index_groups=gr...]
where the time goes in v5:
time: 352 us
  waiting for transfers between devices  243 us (69%)
  Pallas kernels  36.9 us (10%)
  blocking collectives  34.2 us (10%)
  between operations  14.2 us (4%)
  starting transfers between devices  9.04 us (3%)
  matrix products  7.1 us (2%)
  other arithmetic  5.25 us (1%)
    reduce_scatter x1, waiting for transfers between devices, body(): lax.psum_scatter(partial_out.astype(jnp.bfloat16).reshape(n_tp, n_src * t...  103 us
    all_gather x1, waiting for transfers between devices, body(): x_group = lax.all_gather(x_clip, 'tp', axis=0, tiled=False)  91.6 us
    all_to_all x1, blocking collectives, body(): lax.all_to_all(x_mod, 'seq', 0, 0, tiled=True, axis_index_groups=groups)  30.6 us
    ppermute x1, waiting for transfers between devices, body(): other = lax.ppermute(pairs, 'seq', partner)  27.1 us
    all_to_all x1, waiting for transfers between devices, body(): lax.all_to_all(branch_clip, 'seq', 0, 0, tiled=True, axis_index_groups=gr...  22.2 us
    pallas_call x1, Pallas kernels, attend(): pl.pallas_call(kernel, grid=(heads, rows // block_q), in_specs=in_specs,...  19 us
    pallas_call x2, Pallas kernels, project(): pl.pallas_call(kernel, grid=(count,), in_specs=[pl.BlockSpec((rows, width...  17.9 us
  transfers between devices with their start and end apart: 5, of which 4 were waited for; matrix products, arithmetic and copies ran while one was open for 0% of the time, Pallas kernels for 2%

profile of v5, /device:TPU:1, one launch (start us, length us, event | category | flops | bytes accessed | tf_op | source)
XLA Modules:
  0.0 352.1 jit_solution(7606610311290525860)
XLA Ops:
  7.2 0.0 copy-start
  7.2 0.0 copy-start.1
  7.2 0.0 all-gather.3.cloned.1.call-start
  7.2 1.2 slice_bitcast_fusion.1
  8.4 1.3 convert_reduce_fusion.1
  9.8 0.0 copy-done.1
  9.8 0.3 fusion.12
  10.1 0.4 fusion.15
  10.6 0.0 copy-start.4
  10.6 30.6 %all_to_all.10 = bf16[8,16,3072]{2,1,0:T(8,128)(2,1)} all-to-all(bf16[8,16,3072]{2,1,0:T(8,128)(2,1)S(1)} %fusion.15), channel_id=1, replica_groups={{0,8,16,24,32,40,48,56},{64,72,80,88,96,104,112,120},{1,9,17,25,33,41,4..., dimensions={0} | all-to-all | bytes 1572864 | tf_op jit(solution)/shard_map/all_to_all | solution.py:132
  41.2 0.0 all-gather.3.cloned.1.call-update
  41.2 0.0 reduce-scatter.2.cloned.1.call-start
  41.3 0.0 copy-done.4
  41.3 91.6 %all-gather.3.cloned.1.call-done = bf16[64,16,3072]{2,1,0:T(8,128)(2,1)} async-done(((bf16[8,16,3072]{2,1,0:T(8,128)(2,1)}), bf16[64,16,3072]{2,1,0:T(8,128)(2,1)}) %all-gather.3.cloned.1.call-update) | async-done | bytes 6291472 | tf_op jit(solution)/shard_map/all_gather | solution.py:133
  132.9 10.8 %shard_map.113.refs_1_.refs_2_ = bf16[2,1024,384]{2,1,0:T(8,128)(2,1)S(1)} custom-call(bf16[1024,3072]{1,0:T(8,128)(2,1)} %bitcast.69, bf16[3,3072,384]{2,1,0:T(8,128)(2,1)} %bitcast.67, f32[3,128]{1,0:T(4,128)S(1)} %concatenate.3.g_ref), custom_call_target="tpu_custom_call" | custom-call | tf_op jit(solution)/shard_map/pallas_call | solution.py:52
  143.7 0.4 collective-permute-start
  144.1 7.1 %shard_map.112.refs_0_ = bf16[1,1024,384]{2,1,0:T(8,128)(2,1)S(1)} custom-call(bf16[1024,3072]{1,0:T(8,128)(2,1)} %bitcast.70, bf16[3,3072,384]{2,1,0:T(8,128)(2,1)} %bitcast.68, f32[3,128]{1,0:T(4,128)S(1)} %concatenate.3.g_ref), custom_call_target="tpu_custom_call" | custom-call | tf_op jit(solution)/shard_map/pallas_call | solution.py:52
  151.2 27.1 %collective-permute-done.refs_3_.refs_4_ = bf16[2,1024,384]{2,1,0:T(8,128)(2,1)S(1)} collective-permute-done((bf16[2,1024,384]{2,1,0:T(8,128)(2,1)S(1)}, bf16[2,1024,384]{2,1,0:T(8,128)(2,1)S(1)}, u32[]{:S(2)}, u32[]{:S(2)}) %collective-permute-start) | collective-permute-done | bytes 1572896 | tf_op jit(solution)/shard_map/ppermute | solution.py:138
  178.4 19.0 %shard_map.114 = bf16[1024,384]{1,0:T(8,128)(2,1)S(1)} custom-call(bf16[1,1024,384]{2,1,0:T(8,128)(2,1)S(1)} %shard_map.112.refs_0_, bf16[2,1024,384]{2,1,0:T(8,128)(2,1)S(1)} %shard_map.113.refs_1_.refs_2_, bf16[2,1024,384]{2,1,0:T(8,128)(2,1)S(1)} %shard_map.113.refs_1_.refs_2_, bf16[2,1024,384]{2,1,0:T(8,128)(2,1)S(1)} %collective-permute-done.refs_3_.refs_4_, ...), custom_call_target="tpu_custom_call" | custom-call | tf_op jit(solution)/shard_map/pallas_call | solution.py:104
  197.4 0.0 copy-done
  197.4 5.3 %convolution_convert_fusion = bf16[1024,3072]{1,0:T(8,128)(2,1)} fusion(bf16[1024,384]{1,0:T(8,128)(2,1)S(1)} %shard_map.114, bf16[1,384,3072]{2,1,0:T(8,128)(2,1)S(1)} %copy-done), kind=kOutput, calls=%fused_computation | convolution fusion | flops 2419064832 | bytes 9437184 | tf_op jit(solution)/shard_map/re,ed->rd/dot_general | solution.py:141
  202.7 0.0 reduce-scatter.2.cloned.1.call-update
  202.7 0.0 copy-start.3
  202.8 102.6 %reduce-scatter.2.cloned.1.call-done = bf16[1,128,3072]{2,1,0:T(8,128)(2,1)} async-done(((bf16[8,128,3072]{2,1,0:T(8,128)(2,1)}), bf16[1,128,3072]{2,1,0:T(8,128)(2,1)}) %reduce-scatter.2.cloned.1.call-update) | async-done | bytes 786448 | tf_op jit(solution)/shard_map/reduce_scatter | solution.py:144
  305.3 6.8 %all-to-all-start.1 = ((bf16[8,16,3072]{2,1,0:T(8,128)(2,1)}), bf16[8,16,3072]{2,1,0:T(8,128)(2,1)}, u32[]{:S(2)}, u32[]{:S(2)}) async-start(bf16[8,16,3072]{2,1,0:T(8,128)(2,1)} %bitcast.72), calls=%async_computation.2 | async-start | bytes 1572864 | tf_op jit(solution)/shard_map/all_to_all | solution.py:151
  312.1 0.0 copy-done.3
  312.1 0.2 fusion.25
  312.3 22.2 %all-to-all-done.1 = bf16[8,16,3072]{2,1,0:T(8,128)(2,1)} async-done(((bf16[8,16,3072]{2,1,0:T(8,128)(2,1)}), bf16[8,16,3072]{2,1,0:T(8,128)(2,1)}, u32[]{:S(2)}, u32[]{:S(2)}) %all-to-all-start.1) | async-done | bytes 786464 | tf_op jit(solution)/shard_map/all_to_all | solution.py:151
  334.4 0.0 copy-start.5
  334.4 0.0 copy-start.6
  334.5 1.5 convert_reduce_fusion
  336.0 0.0 copy-start.2
  336.0 0.3 fusion.8
  336.4 0.0 copy-done.5
  336.4 0.0 copy-done.6
  336.4 0.5 fusion.23
  336.9 0.1 copy-done.2
  337.0 1.2 fusion
  338.2 1.8 collective-permute-start.1
  340.1 3.6 %psum.7 = bf16[2,8,64,16]{2,3,1,0:T(8,128)(2,1)S(1)} all-reduce(bf16[2,8,64,16]{2,3,1,0:T(8,128)(2,1)S(1)} %maximum_select_fusion), channel_id=1, replica_groups=mesh['comp'=2,'seq'=16,'tp'=8] {'comp'}, use_global_device_ids=true, to_apply=%region_5.6 | all-reduce | flops 16384 | bytes 65536 | tf_op jit(solution)/shard_map/psum | solution.py:15
  343.7 0.7 slice_bitcast_fusion.2
  344.3 0.0 collective-permute-done.1
  344.3 0.9 copy.24
  (8 shorter events, 0.1 us)
Async XLA Ops:
  7.2 190.2 %copy-start = (bf16[1,384,3072]{2,1,0:T(8,128)(2,1)S(1)}, bf16[1,384,3072]{2,1,0:T(8,128)(2,1)}, u32[]{:S(2)}) copy-start(bf16[1,384,3072]{2,1,0:T(8,128)(2,1)} %param.12) | copy-start | bytes 7077892
  7.2 2.6 copy-start.1
  7.2 125.7 %all-gather.3.cloned.1.call-start = ((), (), s32[]{:S(2)}) async-start(), calls=%async_computation.4 | async-start | bytes 7077888 | tf_op jit(solution)/shard_map/all_gather | solution.py:133
  10.6 30.7 %copy-start.4 = (f32[1,2,128]{2,1,0:T(2,128)S(1)}, f32[1,2,128]{2,1,0:T(2,128)}, u32[]{:S(2)}) copy-start(f32[1,2,128]{2,1,0:T(2,128)} %param.13) | copy-start | bytes 3076
  41.2 264.1 %reduce-scatter.2.cloned.1.call-start = ((), (), s32[]{:S(2)}) async-start(), calls=%async_computation.3 | async-start | bytes 7077888 | tf_op jit(solution)/shard_map/reduce_scatter | solution.py:144
  143.7 34.6 %collective-permute-start = (bf16[2,1024,384]{2,1,0:T(8,128)(2,1)S(1)}, bf16[2,1024,384]{2,1,0:T(8,128)(2,1)S(1)}, u32[]{:S(2)}, u32[]{:S(2)}) collective-permute-start(bf16[2,1024,384]{2,1,0:T(8,128)(2,1)S(1)} %shard_map.113.refs_1_.refs_2_), channel_id=1, source_target_pairs={{0,64},{8,72},{16,80},{24,88},{32,96},{40,104},{48,112},{56,120},{... | collective-permute-start | bytes 4718600 | tf_op jit(solution)/shard_map/ppermute | solution.py:138
  202.7 109.3 %copy-start.3 = (f32[8,2,3072]{2,1,0:T(2,128)S(1)}, f32[8,2,3072]{2,1,0:T(2,128)}, u32[]{:S(2)}) copy-start(f32[8,2,3072]{2,1,0:T(2,128)} %param.14) | copy-start | bytes 589828
  305.3 29.1 %all-to-all-start.1 = ((bf16[8,16,3072]{2,1,0:T(8,128)(2,1)}), bf16[8,16,3072]{2,1,0:T(8,128)(2,1)}, u32[]{:S(2)}, u32[]{:S(2)}) async-start(bf16[8,16,3072]{2,1,0:T(8,128)(2,1)} %bitcast.72), calls=%async_computation.2 | async-start | bytes 1572864 | tf_op jit(solution)/shard_map/all_to_all | solution.py:151
  334.4 1.9 copy-start.5
  334.4 1.9 copy-start.6
  336.0 1.0 copy-start.2
  338.2 6.1 %collective-permute-start.1 = (bf16[8,16,3072]{2,1,0:T(8,128)(2,1)}, bf16[8,16,3072]{2,1,0:T(8,128)(2,1)S(1)}, u32[]{:S(2)}, u32[]{:S(2)}) collective-permute-start(bf16[8,16,3072]{2,1,0:T(8,128)(2,1)} %fusion), channel_id=1, source_target_pairs={{128,0},{0,128},{129,1},{1,129},{130,2},{2,130},{131,3},{3,131},{1... | collective-permute-start | bytes 2359304 | tf_op jit(solution)/shard_map/ppermute | solution.py:21
Sparse Core Ops, SparseCore 0:
  41.4 91.5 all-gather.2
  202.9 102.4 reduce-scatter.1

commit v6 on v5

--- a/solution.py
+++ b/solution.py
@@ -109,6 +109,73 @@
         out_shape=jax.ShapeDtypeStruct((rows, width), jnp.bfloat16),
         compiler_params=pltpu.CompilerParams(vmem_limit_bytes=48 * 1024 * 1024),
     )(*operands)
+
+
+def _attend_own_kernel(q_ref, k_ref, v_ref, acc_ref, max_ref, sum_ref, *, scaling):
+    scores = lax.dot_general(
+        q_ref[...], k_ref[...], (((1,), (1,)), ((), ())), preferred_element_type=jnp.float32
+    ) * scaling
+    row_max = jnp.max(scores, -1, keepdims=True)
+    weight = jnp.exp(scores - row_max)
+    row_sum = jnp.sum(weight, -1, keepdims=True)
+    acc_ref[...] = jnp.dot(
+        weight.astype(jnp.bfloat16), v_ref[...], preferred_element_type=jnp.float32
+    )
+    max_ref[...] = jnp.broadcast_to(row_max, max_ref.shape)
+    sum_ref[...] = jnp.broadcast_to(row_sum, sum_ref.shape)
+
+
+def _attend_far_kernel(q_ref, k_ref, v_ref, acc_ref, max_ref, sum_ref, o_ref, *, scaling):
+    scores = lax.dot_general(
+        q_ref[...], k_ref[...], (((1,), (1,)), ((), ())), preferred_element_type=jnp.float32
+    ) * scaling
+    own_max = max_ref[:, :1]
+    row_max = jnp.maximum(own_max, jnp.max(scores, -1, keepdims=True))
+    rescale = jnp.exp(own_max - row_max)
+    weight = jnp.exp(scores - row_max)
+    row_sum = sum_ref[:, :1] * rescale + jnp.sum(weight, -1, keepdims=True)
+    summed = acc_ref[...] * rescale + jnp.dot(
+        weight.astype(jnp.bfloat16), v_ref[...], preferred_element_type=jnp.float32
+    )
+    o_ref[...] = (summed / row_sum).astype(o_ref.dtype)
+
+
+def _attend_specs(queries, pairs, head_dim, block_q):
+    keys = pairs.shape[1]
+    return [
+        pl.BlockSpec((None, block_q, head_dim), lambda h, i: (0, i, h)),
+        pl.BlockSpec((None, keys, head_dim), lambda h, i: (0, 0, h)),
+        pl.BlockSpec((None, keys, head_dim), lambda h, i: (1, 0, h)),
+    ]
+
+
+def attend_own(queries, pairs, head_dim, block_q=512):
+    rows, width = queries.shape[1], queries.shape[2]
+    heads = width // head_dim
+    tile = pl.BlockSpec((block_q, head_dim), lambda h, i: (i, h))
+    stats = jax.ShapeDtypeStruct((rows, width), jnp.float32)
+    return pl.pallas_call(
+        functools.partial(_attend_own_kernel, scaling=head_dim ** (-0.5)),
+        grid=(heads, rows // block_q),
+        in_specs=_attend_specs(queries, pairs, head_dim, block_q),
+        out_specs=[tile, tile, tile],
+        out_shape=[stats, stats, stats],
+        compiler_params=pltpu.CompilerParams(vmem_limit_bytes=48 * 1024 * 1024),
+    )(queries, pairs, pairs)
+
+
+def attend_far(queries, pairs, partial, head_dim, block_q=512):
+    rows, width = queries.shape[1], queries.shape[2]
+    heads = width // head_dim
+    tile = pl.BlockSpec((block_q, head_dim), lambda h, i: (i, h))
+    return pl.pallas_call(
+        functools.partial(_attend_far_kernel, scaling=head_dim ** (-0.5)),
+        grid=(heads, rows // block_q),
+        in_specs=_attend_specs(queries, pairs, head_dim, block_q) + [tile, tile, tile],
+        out_specs=tile,
+        out_shape=jax.ShapeDtypeStruct((rows, width), jnp.bfloat16),
+        compiler_params=pltpu.CompilerParams(vmem_limit_bytes=48 * 1024 * 1024),
+    )(queries, pairs, pairs, *partial)
 
 
 def body(inputs, modulation, w_qkv, w_attn_out, qk_gain, final_mod, w_final, w_embed, latent):
@@ -137,7 +204,8 @@
     pairs = project(x_group, weights, gains, head_dim, 1, 2)
     other = lax.ppermute(pairs, "seq", partner)
     queried = project(x_group, weights, gains, head_dim, 0, 1)
-    attended = attend(queried, [(pairs, 0), (other, 0)], head_dim)
+    partial = attend_own(queried, pairs, head_dim)
+    attended = attend_far(queried, other, partial, head_dim)
     partial_out = jnp.einsum(
         "re,ed->rd", attended, w_attn_out[0], preferred_element_type=jnp.float32
     )
@@ -161,14 +229,16 @@
     advanced = latent + step_size * velocity
     last_comp = lax.axis_size("comp") - 1
     position = lax.axis_index("comp")
-    shared = broadcast(
-        jnp.stack([velocity, advanced]).astype(jnp.bfloat16), "comp", last_comp
-    ).astype(jnp.float32)
+    shared = jnp.stack([velocity, advanced]).astype(jnp.bfloat16)
     embedded = jnp.einsum(
         "scr,cd->srd", advanced.astype(jnp.bfloat16), w_embed, preferred_element_type=jnp.float32
     ).astype(jnp.bfloat16)
     sending = jnp.where(position == last_comp, embedded, output)
-    handed = shifted(sending, "comp", 1)
+    packed = jnp.concatenate([sending.reshape(-1), shared.reshape(-1)])
+    arrived = shifted(packed, "comp", 1)
+    handed = arrived[: sending.size].reshape(sending.shape)
+    from_last = arrived[sending.size :].reshape(shared.shape)
+    shared = jnp.where(position == last_comp, shared, from_last).astype(jnp.float32)
     return (handed[None], shared[0], shared[1])
 
 

time: 352 us -> 350 us (level)
  waiting for transfers between devices: 243 us -> 232 us
  local copies, waits for them, and re-layouts: 1.83 us -> 8.63 us
  Pallas kernels: 36.9 us -> 42.2 us
  blocking collectives: 34.2 us -> 30.6 us
    ppermute x1, waiting for transfers between devices: 27.1 us -> 13.6 us  [body(): other = lax.ppermute(pairs, 'seq', partner)]
    pallas_call x1 -> x2, Pallas kernels: 19 us -> 24.2 us  [the longest x1 13.1 us: attend_far(): pl.pallas_call(functools.partial(_attend_far_kernel, scaling=head_dim **...]
    psum x1 -> x0, blocking collectives: 3.59 us -> none  [broadcast(): return lax.psum(block, axis)]
  transfers between devices with their start and end apart: 5 -> 5, of which waited for: 4 -> 5; matrix products, arithmetic and copies ran while one was open for 0% -> 0% of each run, Pallas kernels for 2% -> 5%
where the time goes in v6:
time: 350 us
  waiting for transfers between devices  232 us (66%)
  Pallas kernels  42.2 us (12%)
  blocking collectives  30.6 us (9%)
  between operations  14.3 us (4%)
  starting transfers between devices  10.2 us (3%)
  local copies, waits for them, and re-layouts  8.63 us (2%)
  matrix products  6.3 us (2%)
  other arithmetic  5.33 us (2%)
    reduce_scatter x1, waiting for transfers between devices, body(): lax.psum_scatter(partial_out.astype(jnp.bfloat16).reshape(n_tp, n_src * t...  103 us
    all_gather x1, waiting for transfers between devices, body(): x_group = lax.all_gather(x_clip, 'tp', axis=0, tiled=False)  91.6 us
    all_to_all x1, blocking collectives, body(): lax.all_to_all(x_mod, 'seq', 0, 0, tiled=True, axis_index_groups=groups)  30.6 us
    all_to_all x1, waiting for transfers between devices, body(): lax.all_to_all(branch_clip, 'seq', 0, 0, tiled=True, axis_index_groups=gr...  22.2 us
    pallas_call x2, Pallas kernels, project(): pl.pallas_call(kernel, grid=(count,), in_specs=[pl.BlockSpec((rows, width...  18 us
    ppermute x1, waiting for transfers between devices, body(): other = lax.ppermute(pairs, 'seq', partner)  13.6 us
    pallas_call x1, Pallas kernels, attend_far(): pl.pallas_call(functools.partial(_attend_far_kernel, scaling=head_dim **...  13.1 us
    pallas_call x1, Pallas kernels, attend_own(): pl.pallas_call(functools.partial(_attend_own_kernel, scaling=head_dim **...  11.1 us
  transfers between devices with their start and end apart: 5, of which 5 were waited for; matrix products, arithmetic and copies ran while one was open for 0% of the time, Pallas kernels for 5%

profile of v6, /device:TPU:1, one launch (start us, length us, event | category | flops | bytes accessed | tf_op | source)
XLA Modules:
  0.0 349.8 jit_solution(11782994634017829319)
XLA Ops:
  7.2 0.0 copy-start
  7.2 0.0 copy-start.4
  7.2 0.0 all-gather.3.cloned.1.call-start
  7.2 1.2 slice_bitcast_fusion.1
  8.4 1.3 convert_reduce_fusion.1
  9.8 0.3 fusion.12
  10.1 0.4 fusion.15
  10.6 0.0 copy-start.9
  10.6 30.6 %all_to_all.10 = bf16[8,16,3072]{2,1,0:T(8,128)(2,1)} all-to-all(bf16[8,16,3072]{2,1,0:T(8,128)(2,1)S(1)} %fusion.15), channel_id=1, replica_groups={{0,8,16,24,32,40,48,56},{64,72,80,88,96,104,112,120},{1,9,17,25,33,41,4..., dimensions={0} | all-to-all | bytes 1572864 | tf_op jit(solution)/shard_map/all_to_all | solution.py:199
  41.2 0.0 all-gather.3.cloned.1.call-update
  41.2 0.0 reduce-scatter.2.cloned.1.call-start
  41.3 91.6 %all-gather.3.cloned.1.call-done = bf16[64,16,3072]{2,1,0:T(8,128)(2,1)} async-done(((bf16[8,16,3072]{2,1,0:T(8,128)(2,1)}), bf16[64,16,3072]{2,1,0:T(8,128)(2,1)}) %all-gather.3.cloned.1.call-update) | async-done | bytes 6291472 | tf_op jit(solution)/shard_map/all_gather | solution.py:200
  132.9 10.8 %shard_map.113.k_ref.v_ref = bf16[2,1024,384]{2,1,0:T(8,128)(2,1)S(1)} custom-call(bf16[1024,3072]{1,0:T(8,128)(2,1)} %bitcast.72, bf16[3,3072,384]{2,1,0:T(8,128)(2,1)} %bitcast.70, f32[3,128]{1,0:T(4,128)S(1)} %concatenate.6.g_ref), custom_call_target="tpu_custom_call" | custom-call | tf_op jit(solution)/shard_map/pallas_call | solution.py:52
  143.7 0.4 collective-permute-start
  144.1 7.2 %shard_map.112.q_ref = bf16[1,1024,384]{2,1,0:T(8,128)(2,1)S(1)} custom-call(bf16[1024,3072]{1,0:T(8,128)(2,1)} %bitcast.73, bf16[3,3072,384]{2,1,0:T(8,128)(2,1)} %bitcast.71, f32[3,128]{1,0:T(4,128)S(1)} %concatenate.6.g_ref), custom_call_target="tpu_custom_call" | custom-call | tf_op jit(solution)/shard_map/pallas_call | solution.py:52
  151.4 11.1 %shard_map.114 = (f32[1024,384]{1,0:T(8,128)S(1)}, f32[1024,384]{1,0:T(8,128)S(1)}, f32[1024,384]{1,0:T(8,128)S(1)}) custom-call(bf16[1,1024,384]{2,1,0:T(8,128)(2,1)S(1)} %shard_map.112.q_ref, bf16[2,1024,384]{2,1,0:T(8,128)(2,1)} %copy-done.1, bf16[2,1024,384]{2,1,0:T(8,128)(2,1)} %copy-done.1), custom_call_target="tpu_custom_call" | custom-call | tf_op jit(solution)/shard_map/pallas_call | solution.py:157
  162.5 1.2 copy-done.2
  163.7 1.1 copy-done.3
  164.8 13.6 %collective-permute-done.k_ref.v_ref = bf16[2,1024,384]{2,1,0:T(8,128)(2,1)S(1)} collective-permute-done((bf16[2,1024,384]{2,1,0:T(8,128)(2,1)S(1)}, bf16[2,1024,384]{2,1,0:T(8,128)(2,1)S(1)}, u32[]{:S(2)}, u32[]{:S(2)}) %collective-permute-start) | collective-permute-done | bytes 1572896 | tf_op jit(solution)/shard_map/ppermute | solution.py:205
  178.4 13.1 %shard_map.115 = bf16[1024,384]{1,0:T(8,128)(2,1)S(1)} custom-call(bf16[1,1024,384]{2,1,0:T(8,128)(2,1)S(1)} %shard_map.112.q_ref, bf16[2,1024,384]{2,1,0:T(8,128)(2,1)S(1)} %collective-permute-done.k_ref.v_ref, bf16[2,1024,384]{2,1,0:T(8,128)(2,1)S(1)} %collective-permute-done.k_ref.v_ref, f32[1024,384]{1,0:T(8,128)S(1)} %get-tuple-element.6.acc_ref, ...), custom_call_target="tpu_custom_call" | custom-call | tf_op jit(solution)/shard_map/pallas_call | solution.py:171
  191.5 5.4 %convolution_convert_fusion = bf16[1024,3072]{1,0:T(8,128)(2,1)} fusion(bf16[1024,384]{1,0:T(8,128)(2,1)S(1)} %shard_map.115, bf16[1,384,3072]{2,1,0:T(8,128)(2,1)S(1)} %copy-done), kind=kOutput, calls=%fused_computation | convolution fusion | flops 2419064832 | bytes 9437184 | tf_op jit(solution)/shard_map/re,ed->rd/dot_general | solution.py:209
  196.9 0.0 reduce-scatter.2.cloned.1.call-update
  196.9 0.0 copy-start.8
  196.9 102.7 %reduce-scatter.2.cloned.1.call-done = bf16[1,128,3072]{2,1,0:T(8,128)(2,1)} async-done(((bf16[8,128,3072]{2,1,0:T(8,128)(2,1)}), bf16[1,128,3072]{2,1,0:T(8,128)(2,1)}) %reduce-scatter.2.cloned.1.call-update) | async-done | bytes 786448 | tf_op jit(solution)/shard_map/reduce_scatter | solution.py:212
  299.6 6.7 %all-to-all-start.1 = ((bf16[8,16,3072]{2,1,0:T(8,128)(2,1)}), bf16[8,16,3072]{2,1,0:T(8,128)(2,1)}, u32[]{:S(2)}, u32[]{:S(2)}) async-start(bf16[8,16,3072]{2,1,0:T(8,128)(2,1)} %bitcast.79), calls=%async_computation.2 | async-start | bytes 1572864 | tf_op jit(solution)/shard_map/all_to_all | solution.py:219
  306.4 0.2 fusion.29
  306.6 22.2 %all-to-all-done.1 = bf16[8,16,3072]{2,1,0:T(8,128)(2,1)} async-done(((bf16[8,16,3072]{2,1,0:T(8,128)(2,1)}), bf16[8,16,3072]{2,1,0:T(8,128)(2,1)}, u32[]{:S(2)}, u32[]{:S(2)}) %all-to-all-start.1) | async-done | bytes 786464 | tf_op jit(solution)/shard_map/all_to_all | solution.py:219
  328.8 1.5 convert_reduce_fusion
  330.3 0.0 copy-start.5
  330.4 0.0 copy-start.7
  330.4 0.3 fusion.8
  330.7 0.0 copy-start.6
  330.8 0.5 fusion.17
  331.3 0.0 copy-done.7
  331.3 0.2 copy.19
  331.5 0.2 convert_element_type.51
  331.7 0.0 copy-done.6
  331.8 0.3 fusion
  332.1 0.2 copy.23
  332.3 0.1 pad_maximum_fusion
  332.3 2.9 collective-permute-start.1
  335.3 2.1 collective-permute-done.1
  337.4 1.2 slice.47
  338.6 1.2 broadcast_in_dim_reshape.3
  339.8 1.4 slice.48
  341.2 1.0 reshape.61
  342.1 0.1 copy.20
  342.3 0.7 slice_bitcast_fusion.2
  (20 shorter events, 0.2 us)
Async XLA Ops:
  7.2 184.3 %copy-start = (bf16[1,384,3072]{2,1,0:T(8,128)(2,1)S(1)}, bf16[1,384,3072]{2,1,0:T(8,128)(2,1)}, u32[]{:S(2)}) copy-start(bf16[1,384,3072]{2,1,0:T(8,128)(2,1)} %param.12) | copy-start | bytes 7077892
  7.2 2.6 copy-start.4
  7.2 125.7 %all-gather.3.cloned.1.call-start = ((), (), s32[]{:S(2)}) async-start(), calls=%async_computation.4 | async-start | bytes 7077888 | tf_op jit(solution)/shard_map/all_gather | solution.py:200
  10.6 30.7 %copy-start.9 = (f32[1,2,128]{2,1,0:T(2,128)S(1)}, f32[1,2,128]{2,1,0:T(2,128)}, u32[]{:S(2)}) copy-start(f32[1,2,128]{2,1,0:T(2,128)} %param.13) | copy-start | bytes 3076
  41.2 258.4 %reduce-scatter.2.cloned.1.call-start = ((), (), s32[]{:S(2)}) async-start(), calls=%async_computation.3 | async-start | bytes 7077888 | tf_op jit(solution)/shard_map/reduce_scatter | solution.py:212
  143.7 7.7 %copy-start.1 = (bf16[2,1024,384]{2,1,0:T(8,128)(2,1)}, bf16[2,1024,384]{2,1,0:T(8,128)(2,1)S(1)}, u32[]{:S(2)}) copy-start(bf16[2,1024,384]{2,1,0:T(8,128)(2,1)S(1)} %shard_map.113.k_ref.v_ref) | copy-start | bytes 4718596
  143.7 34.6 %collective-permute-start = (bf16[2,1024,384]{2,1,0:T(8,128)(2,1)S(1)}, bf16[2,1024,384]{2,1,0:T(8,128)(2,1)S(1)}, u32[]{:S(2)}, u32[]{:S(2)}) collective-permute-start(bf16[2,1024,384]{2,1,0:T(8,128)(2,1)S(1)} %shard_map.113.k_ref.v_ref), channel_id=1, source_target_pairs={{0,64},{8,72},{16,80},{24,88},{32,96},{40,104},{48,112},{56,120},{... | collective-permute-start | bytes 4718600 | tf_op jit(solution)/shard_map/ppermute | solution.py:205
  162.5 1.2 copy-start.2
  163.7 1.1 copy-start.3
  196.9 109.4 %copy-start.8 = (f32[8,2,3072]{2,1,0:T(2,128)S(1)}, f32[8,2,3072]{2,1,0:T(2,128)}, u32[]{:S(2)}) copy-start(f32[8,2,3072]{2,1,0:T(2,128)} %param.14) | copy-start | bytes 589828
  299.6 29.2 %all-to-all-start.1 = ((bf16[8,16,3072]{2,1,0:T(8,128)(2,1)}), bf16[8,16,3072]{2,1,0:T(8,128)(2,1)}, u32[]{:S(2)}, u32[]{:S(2)}) async-start(bf16[8,16,3072]{2,1,0:T(8,128)(2,1)} %bitcast.79), calls=%async_computation.2 | async-start | bytes 1572864 | tf_op jit(solution)/shard_map/all_to_all | solution.py:219
  328.8 1.9 copy-start.10
  330.3 0.9 copy-start.5
  330.4 0.9 copy-start.7
  330.7 1.0 copy-start.6
  332.3 5.0 %collective-permute-start.1 = (bf16[409600]{0:T(1024)(128)(2,1)S(1)}, bf16[409600]{0:T(1024)(128)(2,1)}, u32[]{:S(2)}, u32[]{:S(2)}) collective-permute-start(bf16[409600]{0:T(1024)(128)(2,1)S(1)} %pad_maximum_fusion), channel_id=1, source_target_pairs={{128,0},{0,128},{129,1},{1,129},{130,2},{2,130},{131,3},{3,131},{1... | collective-permute-start | bytes 2457608 | tf_op jit(solution)/shard_map/ppermute | solution.py:21
Sparse Core Ops, SparseCore 0:
  41.4 91.5 all-gather.2
  197.0 102.5 reduce-scatter.1
